TPU v7x, 32 devices: a whole 2x2x4 slice. The times are simulated.
32 devices in a mesh: sample: 16 (over z, x, core), block: 2 (over y).
Axes of the slice: x: 2, y: 2, z: 4, core: 2. Of those that a mesh axis runs over, the one named last changes fastest.
Arguments:
- genotype: int32 [16384, 2000], P('sample', 'block'), may hold values from 0 to 2
- allele_freq: float32 [2000], P('block'), may hold values from 0.05 to 0.5
- phenotype: bfloat16 [16384, 16], P('sample'), may hold values from -6 to 6
- shrinkage: float32 [2], replicated, may hold values from 0.05 to 2
- owner_order: int32 [16], replicated, may hold values from 0 to 15, each once
Outputs:
- predictions: bfloat16 [16, 8, 16384], P('block', None, 'sample')
Inputs may be any that keep to these rules, and one draw needn't show every extreme that they name: `owner_order`: each phenotype appears once.
All inputs are finite; a program needn't handle non-finite values.
Results may differ from a plain program's by a relative error of at most 0.0056.
Values may be sent and summed in bfloat16 or wider, within the bound.
No kernel may reach another device: no remote copies, remote signals or barrier semaphores. Data moves between devices by JAX's collectives and lax.ppermute only.
A program may use at most 128 MiB of HBM per device.

v0:
```python
import jax
import jax.numpy as jnp
from jax import lax
from jax.sharding import PartitionSpec as P

SNPS = 500
FOLDS = 5


def standardize(genotype, allele_freq):
    spread = jnp.sqrt(2.0 * allele_freq * (1.0 - allele_freq))
    return ((genotype.astype(jnp.float32) - 2.0 * allele_freq) / spread).astype(jnp.bfloat16)


def solve_pair(factor, target):
    return jax.scipy.linalg.cho_solve((factor, True), target)


def predict(columns, weights):
    stacked = jnp.transpose(weights, (2, 0, 1)).reshape(-1, weights.shape[1])
    product = lax.dot_general(
        stacked, columns, (((1,), (1,)), ((), ())), preferred_element_type=jnp.float32
    )
    return product.astype(jnp.bfloat16).reshape(
        weights.shape[2], weights.shape[0], columns.shape[0]
    )


def inner_products(left_cols, right_cols):
    return lax.dot_general(
        left_cols, right_cols, (((0,), (0,)), ((), ())), preferred_element_type=jnp.float32
    )


def tile_pairs():
    pairs = []
    for row_tile in range(4):
        for col_tile in range(row_tile, 4):
            pairs.append((row_tile, col_tile))
    return pairs


def tile_grams(left_cols, right_cols, tile_width):
    tile_list = []
    for row_tile, col_tile in tile_pairs():
        first = left_cols[:, row_tile * tile_width : (row_tile + 1) * tile_width]
        second = right_cols[:, col_tile * tile_width : (col_tile + 1) * tile_width]
        tile_list.append(inner_products(first, second))
    return jnp.stack(tile_list)


def rebuild(tile_stack):
    pairs = tile_pairs()
    band_rows = []
    for row_tile in range(4):
        band_row = []
        for col_tile in range(4):
            if row_tile <= col_tile:
                band_row.append(tile_stack[pairs.index((row_tile, col_tile))])
            else:
                band_row.append(jnp.transpose(tile_stack[pairs.index((col_tile, row_tile))]))
        band_rows.append(jnp.concatenate(band_row, axis=1))
    return jnp.concatenate(band_rows, axis=0)


def shared_solve(rest_grams, rest_crosses, shrinkage, counts):
    member_count = rest_grams.shape[1]
    width = rest_grams.shape[-1]
    traits = rest_crosses.shape[-1]
    ridge_count = shrinkage.shape[0]
    systems = FOLDS * member_count * ridge_count
    devices = lax.axis_size("sample")
    share = -(-systems // devices)
    flat_grams = rest_grams.reshape(FOLDS * member_count, width, width)
    flat_crosses = rest_crosses.reshape(FOLDS * member_count, width, traits)
    flat_counts = jnp.repeat(counts, member_count)
    owned_ids = lax.axis_index("sample") * share + lax.broadcasted_iota(jnp.int32, (share,), 0)
    owned_ids = jnp.minimum(owned_ids, systems - 1)
    pair_ids = owned_ids // ridge_count
    ridge_ids = owned_ids % ridge_count
    chosen_counts = jnp.take(flat_counts, pair_ids, axis=0)
    system = jnp.take(flat_grams, pair_ids, axis=0) / chosen_counts[:, None, None]
    target = jnp.take(flat_crosses, pair_ids, axis=0) / chosen_counts[:, None, None]
    identity = jnp.eye(width, dtype=jnp.float32)
    full = system + jnp.take(shrinkage, ridge_ids, axis=0)[:, None, None] * identity
    factor = jnp.linalg.cholesky(full)
    solved = jax.vmap(solve_pair, (0, 0))(factor, target).astype(jnp.bfloat16)
    collected = lax.all_gather(solved, "sample", axis=0, tiled=True)
    return collected[:systems].reshape(FOLDS, member_count, ridge_count, width, traits)


def shards(genotype, allele_freq, phenotype, shrinkage, owner_order):
    sample_rows = genotype.shape[0]
    total_rows = sample_rows * lax.axis_size("sample")
    scaled = standardize(genotype, allele_freq)
    ordered = jnp.take(phenotype, owner_order, axis=1)
    local_blocks = allele_freq.shape[0] // SNPS
    tile_width = SNPS // 4
    column_sets = [scaled[:, member * SNPS : (member + 1) * SNPS] for member in range(local_blocks)]
    bounds = [-(-(k * total_rows) // FOLDS) for k in range(FOLDS + 1)]
    counts = jnp.array(
        [float(total_rows - (bounds[k + 1] - bounds[k])) for k in range(FOLDS)], dtype=jnp.float32
    )
    start_row = lax.axis_index("sample") * sample_rows
    row_ids = start_row + lax.broadcasted_iota(jnp.int32, (sample_rows,), 0)
    fold_of = row_ids * FOLDS // total_rows
    first_fold = start_row * FOLDS // total_rows
    slot_folds = [first_fold, first_fold + 1]
    slot_masks = [fold_of == slot_folds[0], fold_of == slot_folds[1]]
    picked = jnp.minimum(jnp.stack(slot_folds), FOLDS - 1)
    fold_ids = jnp.arange(FOLDS, dtype=jnp.int32)

    def fold_partials(member):
        columns = column_sets[member]
        gram_total = jnp.zeros((FOLDS, 10, tile_width, tile_width), jnp.float32)
        cross_total = jnp.zeros((FOLDS, SNPS, ordered.shape[1]), jnp.float32)
        for slot in range(2):
            masked = jnp.where(slot_masks[slot][:, None], columns, jnp.zeros_like(columns))
            selector = (fold_ids == slot_folds[slot]).astype(jnp.float32)
            gram_total = (
                gram_total
                + selector[:, None, None, None] * tile_grams(masked, columns, tile_width)[None]
            )
            cross_total = (
                cross_total + selector[:, None, None] * inner_products(masked, ordered)[None]
            )
        return (gram_total, cross_total)

    def weights_for(members):
        parts = [fold_partials(member) for member in members]
        grams = jnp.stack([item[0] for item in parts], axis=1)
        crosses = jnp.stack([item[1] for item in parts], axis=1)
        summed_grams, summed_crosses = lax.psum((grams, crosses), "sample")
        whole = jax.vmap(jax.vmap(rebuild))(summed_grams)
        rest_grams = jnp.sum(whole, axis=0)[None] - whole
        rest_crosses = jnp.sum(summed_crosses, axis=0)[None] - summed_crosses
        every_weights = shared_solve(rest_grams, rest_crosses, shrinkage, counts)
        return jnp.take(every_weights, picked, axis=0)

    def fold_predictions(member, slot_weights):
        columns = column_sets[member]
        lower = predict(columns, slot_weights[0])
        upper = predict(columns, slot_weights[1])
        return jnp.where(slot_masks[1][None, None, :], upper, lower)

    weights = weights_for(list(range(local_blocks)))
    local_preds = jnp.concatenate(
        [fold_predictions(member, weights[:, member]) for member in range(local_blocks)], axis=1
    )
    return lax.all_to_all(local_preds, "block", split_axis=0, concat_axis=1, tiled=True)


def solution(mesh):
    in_specs = (P("sample", "block"), P("block"), P("sample", None), P(), P())
    out_specs = P("block", None, "sample")
    return jax.shard_map(shards, mesh=mesh, in_specs=in_specs, out_specs=out_specs, check_vma=False)
```

profile of v0, /device:TPU:0, one launch (start us, length us, event | category | flops | bytes accessed | tf_op | source)
XLA Modules:
  0.0 596.6 jit_solution(1321422785324491491)
XLA Ops:
  8.6 2.7 divide_convert_fusion
  31.1 3.5 pad_maximum_fusion
  40.3 146.0 %all-reduce.6.cloned.1.call-done = (f32[5,2,10,125,125]{4,3,1,0,2:T(8,128)}, f32[5,2,500,16]{2,3,1,0:T(8,128)}) async-done(((f32[5,2,10,125,125]{4,3,1,0,2:T(8,128)}, f32[5,2,500,16]{2,3,1,0:T(8,128)}), (f32[5,2,10,125,125]{4,3,1,0,2:T(8,128)}, f32[5,2,500,16]{2,3,1,0:T(8,128)})) %all-reduce.6.cloned.1.call-update) | async-done | bytes 6570016 | tf_op jit(solution)/shard_map/psum | solution.py:133
  186.3 7.2 %slice_bitcast_fusion.19 = (f32[5,2,125,125]{3,2,1,0:T(8,128)}, f32[5,2,125,125]{3,2,1,0:T(8,128)}, f32[5,2,125,125]{2,3,1,0:T(8,128)}, f32[5,2,125,125]{3,2,1,0...) fusion(f32[5,2,10,125,125]{4,3,1,0,2:T(8,128)} %get-tuple-eleme, ...), kind=kLoop, calls=%fused_computation.355 | loop fusion | bytes 18125000 | tf_op jit(solution)/shard_map/vmap(vmap())/squeeze | solution.py:59
  193.4 2.2 slice.448
  197.1 2.2 copy.244
  201.1 2.2 copy.306
  203.3 2.2 copy.250
  205.5 2.2 copy.307
  207.7 3.1 pad_maximum_fusion.1
  210.8 3.3 copy.246
  214.2 12.1 %maximum_reduce_fusion = f32[2,500,500]{2,1,0:T(8,128)S(1)} fusion(f32[5,2,125,125]{3,2,1,0:T(8,128)} %get-tuple-element.37, f32[5,2,125,125]{3,2,1,0:T(8,128)} %copy.245, f32[5,2,125,125]{3,2,1,0:T(8,128)S(1)} %bitcast.329, f32[5,2,125,125]{3,2,1,0:T(8,128)} %copy.244, f32[5,2,125,125]{3,2,1,0:T(8,128)} %get-tuple-element.33, ...), kind=kLoop, calls=%fused_computation.8 | loop fusion | flops 32000000 | bytes 12000000 | tf_op jit(solution)/shard_map/reduce_sum | solution.py:135
  226.5 43.5 %maximum_subtract_fusion = f32[10,500,500]{2,1,0:T(8,128)} fusion(f32[10,125,125]{2,1,0:T(8,128)S(1)} %bitcast.345, f32[10,125,125]{2,1,0:T(8,128)S(1)} %bitcast.338, f32[10,125,125]{2,1,0:T(8,128)S(1)} %bitcast.330, f32[10,125,125]{2,1,0:T(8,128)S(1)} %bitcast.339, f32[10,125,125]{2,1,0:T(8,128)S(1)} %bitcast.344, f32[10,125,125]{2,1,0:T(8,128)S(1)} %bitcast.343, ...), kind=kLoop, calls=%fused_computation.9 | loop fusion | flops 40000000 | bytes 22000000 | tf_op jit(solution)/shard_map/sub | solution.py:135
  270.0 5.9 gather_fusion
  275.9 3.2 select_divide_fusion
  279.1 3.0 copy.256
  282.1 3.4 fusion.1
  286.9 23.6 %custom-call.38 = f32[2,128,128]{2,1,0:T(8,128)S(1)} custom-call(f32[2,128,128]{2,1,0:T(8,128)S(1)} %copy.257), custom_call_target="Cholesky" | custom-call | tf_op jit(solution)/shard_map/jit(cholesky)/cholesky | solution.py:86
  312.1 19.7 %custom-call.39 = f32[2,1,128,128]{2,3,1,0:T(8,128)S(1)} custom-call(f32[2,1,128,128]{3,2,1,0:T(8,128)S(1)} %select_bitcast_fusion.2), custom_call_target="InvertDiagBlocksLowerTriangular" | custom-call | tf_op jit(solution)/shard_map/jit(cholesky)/cholesky | solution.py:86
  331.8 2.6 constant_dynamic-update-slice_fusion.3
  336.1 23.5 %custom-call.40 = f32[2,128,128]{2,1,0:T(8,128)S(1)} custom-call(f32[2,128,128]{2,1,0:T(8,128)S(1)} %copy.262), custom_call_target="Cholesky" | custom-call | tf_op jit(solution)/shard_map/jit(cholesky)/cholesky | solution.py:86
  360.3 19.9 %custom-call.41 = f32[2,1,128,128]{2,3,1,0:T(8,128)S(1)} custom-call(f32[2,1,128,128]{3,2,1,0:T(8,128)S(1)} %get-tuple-element.59), custom_call_target="InvertDiagBlocksLowerTriangular" | custom-call | tf_op jit(solution)/shard_map/jit(cholesky)/cholesky | solution.py:86
  383.5 23.5 %custom-call.42 = f32[2,128,128]{2,1,0:T(8,128)S(1)} custom-call(f32[2,128,128]{2,1,0:T(8,128)S(1)} %copy.267), custom_call_target="Cholesky" | custom-call | tf_op jit(solution)/shard_map/jit(cholesky)/cholesky | solution.py:86
  407.7 19.7 %custom-call.43 = f32[2,1,128,128]{2,3,1,0:T(8,128)S(1)} custom-call(f32[2,1,128,128]{3,2,1,0:T(8,128)S(1)} %get-tuple-element.57), custom_call_target="InvertDiagBlocksLowerTriangular" | custom-call | tf_op jit(solution)/shard_map/jit(cholesky)/cholesky | solution.py:86
  430.3 21.5 %custom-call.44 = f32[2,116,116]{2,1,0:T(8,128)S(1)} custom-call(f32[2,116,116]{2,1,0:T(8,128)S(1)} %copy.271), custom_call_target="Cholesky" | custom-call | tf_op jit(solution)/shard_map/jit(cholesky)/cholesky | solution.py:86
  456.4 9.2 %while.1 = (s32[]{:T(128)}, f32[2,500,500]{2,1,0:T(8,128)}, s32[3,2]{0,1:T(2,128)S(1)}, f32[3,2,128,128]{3,2,0,1:T(8,128)S(1)}, s32[]{:T(128)}) while((s32[]{:T(128)}, f32[2,500,500]{2,1,0:T(8,128)}, s32[3,2]{0,1:T(2,128)S(1)}, f32[3,2,128,128]{3,2,0,1:T(8,128)S(1)}, s32[]{:T(128)}) %tuple.71), condition=%wide.while_cond, body=%wide.while_body.sunk | while | flops 2 | bytes 262261 | solution.py:16
  457.0 2.4 bitcast_dynamic-update-slice_fusion.2
  460.1 2.4 bitcast_dynamic-update-slice_fusion.2
  463.2 2.4 bitcast_dynamic-update-slice_fusion.2
  466.6 79.4 %custom-call.45 = f32[2,4,128,128]{2,3,1,0:T(8,128)S(1)} custom-call(f32[2,4,128,128]{3,2,1,0:T(8,128)} %pad_maximum_fusion.2), custom_call_target="InvertDiagBlocksLowerTriangular" | custom-call | tf_op jit(solution)/shard_map/vmap(jit(_cho_solve))/triangular_solve | solution.py:16
  556.8 21.9 %all_gather.3 = bf16[32,500,16]{1,2,0:T(8,128)(2,1)S(1)} all-gather(bf16[2,500,16]{1,2,0:T(8,128)(2,1)S(1)} %pad_maximum_fusion.5), channel_id=1, replica_groups=mesh['sample'=16,'block'=2] {'sample'}, dimensions={0}, use_global_device_ids=true | all-gather | bytes 544000 | tf_op jit(solution)/shard_map/all_gather | solution.py:88
  581.6 7.0 %all_to_all.18 = bf16[16,4,1024]{2,1,0:T(4,128)(2,1)S(1)} all-to-all(bf16[16,4,1024]{2,1,0:T(4,128)(2,1)S(1)} %pad_maximum_fusion.4), channel_id=1, replica_groups=mesh['sample'=16,'block'=2] {'block'}, dimensions={0} | all-to-all | bytes 262144 | tf_op jit(solution)/shard_map/all_to_all | solution.py:150
  (221 shorter events, 64.5 us)
Async XLA Ops:
  6.5 8.1 %copy-start = (bf16[1024,16]{0,1:T(8,128)(2,1)S(1)}, bf16[1024,16]{0,1:T(8,128)(2,1)}, u32[]{:S(2)}) copy-start(bf16[1024,16]{0,1:T(8,128)(2,1)} %param.8) | copy-start | bytes 98308
  6.5 179.7 %all-reduce.6.cloned.1.call-start = ((), (), s32[]{:S(2)}) async-start(), calls=%async_computation.1 | async-start | bytes 13762560 | tf_op jit(solution)/shard_map/psum | solution.py:133
  12.6 2.0 copy-start.15
  12.6 2.0 copy-start.17
  15.2 3.3 copy-start.14
  18.6 1.3 copy-start.18
  18.6 1.4 copy-start.29
  21.8 1.2 copy-start.16
  21.8 1.4 copy-start.28
  35.5 0.8 copy-start.2
  193.4 5.9 copy-start.7
  214.1 12.2 %copy-start.4 = (f32[5,2,1,125,125]{4,3,1,0,2:T(8,128)S(1)}, f32[5,2,1,125,125]{4,3,1,0,2:T(8,128)}, u32[]{:S(2)}) copy-start(f32[5,2,1,125,125]{4,3,1,0,2:T(8,128)} %get-tuple-element.38) | copy-start | bytes 1875004
  214.1 12.3 %copy-start.5 = (f32[5,2,1,125,125]{4,3,1,0,2:T(8,128)S(1)}, f32[5,2,1,125,125]{4,3,1,0,2:T(8,128)}, u32[]{:S(2)}) copy-start(f32[5,2,1,125,125]{4,3,1,0,2:T(8,128)} %get-tuple-element.39) | copy-start | bytes 1875004
  214.1 12.3 %copy-start.6 = (f32[5,2,1,125,125]{4,3,1,0,2:T(8,128)S(1)}, f32[5,2,1,125,125]{4,3,1,0,2:T(8,128)}, u32[]{:S(2)}) copy-start(f32[5,2,1,125,125]{4,3,1,0,2:T(8,128)} %get-tuple-element.40) | copy-start | bytes 1875004
  214.1 12.3 %copy-start.8 = (f32[5,2,1,125,125]{4,3,1,0,2:T(8,128)S(1)}, f32[5,2,1,125,125]{4,3,1,0,2:T(8,128)}, u32[]{:S(2)}) copy-start(f32[5,2,1,125,125]{4,3,1,0,2:T(8,128)} %copy-done.7) | copy-start | bytes 1875004
  214.1 12.3 %copy-start.9 = (f32[5,2,125,125]{3,2,1,0:T(8,128)S(1)}, f32[5,2,125,125]{3,2,1,0:T(8,128)}, u32[]{:S(2)}) copy-start(f32[5,2,125,125]{3,2,1,0:T(8,128)} %copy.245) | copy-start | bytes 1875004
  214.1 12.3 %copy-start.10 = (f32[5,2,125,125]{3,2,1,0:T(8,128)S(1)}, f32[5,2,125,125]{3,2,1,0:T(8,128)}, u32[]{:S(2)}) copy-start(f32[5,2,125,125]{3,2,1,0:T(8,128)} %copy.244) | copy-start | bytes 1875004
  214.1 12.3 %copy-start.11 = (f32[5,2,1,125,125]{3,4,1,0,2:T(8,128)S(1)}, f32[5,2,1,125,125]{3,4,1,0,2:T(8,128)}, u32[]{:S(2)}) copy-start(f32[5,2,1,125,125]{3,4,1,0,2:T(8,128)} %copy.306) | copy-start | bytes 1875004
  214.2 12.3 %copy-start.19 = (f32[5,2,1,125,125]{4,3,1,0,2:T(8,128)S(1)}, f32[5,2,1,125,125]{4,3,1,0,2:T(8,128)}, u32[]{:S(2)}) copy-start(f32[5,2,1,125,125]{4,3,1,0,2:T(8,128)} %get-tuple-element.41) | copy-start | bytes 1875004
  214.2 12.3 %copy-start.20 = (f32[5,2,1,125,125]{4,3,1,0,2:T(8,128)S(1)}, f32[5,2,1,125,125]{4,3,1,0,2:T(8,128)}, u32[]{:S(2)}) copy-start(f32[5,2,1,125,125]{4,3,1,0,2:T(8,128)} %get-tuple-element.42) | copy-start | bytes 1875004
  214.2 12.3 %copy-start.21 = (f32[5,2,1,125,125]{4,3,1,0,2:T(8,128)S(1)}, f32[5,2,1,125,125]{4,3,1,0,2:T(8,128)}, u32[]{:S(2)}) copy-start(f32[5,2,1,125,125]{4,3,1,0,2:T(8,128)} %get-tuple-element.43) | copy-start | bytes 1875004
  214.2 12.3 %copy-start.22 = (f32[5,2,1,125,125]{4,3,1,0,2:T(8,128)S(1)}, f32[5,2,1,125,125]{4,3,1,0,2:T(8,128)}, u32[]{:S(2)}) copy-start(f32[5,2,1,125,125]{4,3,1,0,2:T(8,128)} %get-tuple-element.44) | copy-start | bytes 1875004
  214.2 12.3 %copy-start.23 = (f32[5,2,1,125,125]{4,3,1,0,2:T(8,128)S(1)}, f32[5,2,1,125,125]{4,3,1,0,2:T(8,128)}, u32[]{:S(2)}) copy-start(f32[5,2,1,125,125]{4,3,1,0,2:T(8,128)} %get-tuple-element.46) | copy-start | bytes 1875004
  214.2 12.3 %copy-start.24 = (f32[5,2,1,125,125]{4,3,1,0,2:T(8,128)S(1)}, f32[5,2,1,125,125]{4,3,1,0,2:T(8,128)}, u32[]{:S(2)}) copy-start(f32[5,2,1,125,125]{4,3,1,0,2:T(8,128)} %slice.448) | copy-start | bytes 1875004
  214.2 12.3 %copy-start.25 = (f32[5,2,125,125]{3,2,1,0:T(8,128)S(1)}, f32[5,2,125,125]{3,2,1,0:T(8,128)}, u32[]{:S(2)}) copy-start(f32[5,2,125,125]{3,2,1,0:T(8,128)} %copy.250) | copy-start | bytes 1875004
  279.1 3.0 copy-start.13
  285.5 1.3 copy-start.12
  381.5 71.5 %copy-start.27 = (pred[500,500]{1,0:T(8,128)(4,1)S(1)}, pred[500,500]{1,0:T(8,128)(4,1)}, u32[]{:S(2)}) copy-start(pred[500,500]{1,0:T(8,128)(4,1)} %iota_compare_fusion.2) | copy-start | bytes 750004
  453.0 3.3 copy-start.30
  455.0 1.3 copy-start.3
  455.0 91.0 %copy-start.26 = (f32[5,2,500,16]{2,3,1,0:T(8,128)S(1)}, f32[5,2,500,16]{2,3,1,0:T(8,128)}, u32[]{:S(2)}) copy-start(f32[5,2,500,16]{2,3,1,0:T(8,128)} %get-tuple-element.25) | copy-start | bytes 960004
  580.8 8.5 %copy-start.1 = (bf16[1024,16]{0,1:T(8,128)(2,1)S(1)}, bf16[1024,16]{0,1:T(8,128)(2,1)}, u32[]{:S(2)}) copy-start(bf16[1024,16]{0,1:T(8,128)(2,1)} %param.8) | copy-start | bytes 98308
  (1 other events, 0.7 us)
Sparse Core Ops, SparseCore 0:
  35.7 150.5 all-reduce.5
where the time goes:
time: 606 us; the launch traced here: 597 us
  other arithmetic  316 us (52%)
  waiting for transfers between devices  146 us (24%)
  local copies, waits for them, and re-layouts  53.5 us (9%)
  matrix products  37.2 us (6%)
  blocking collectives  28.9 us (5%)
  between operations  14.9 us (2%)
    another operation x18, other arithmetic, shared_solve(): factor = jnp.linalg.cholesky(full)  154 us
    psum x1, waiting for transfers between devices, weights_for(): summed_grams, summed_crosses = lax.psum((grams, crosses), 'sample')  146 us
    another operation x9, other arithmetic, solve_pair(): return jax.scipy.linalg.cho_solve((factor, True), target)  83.2 us
    sub x1, other arithmetic, weights_for(): rest_grams = jnp.sum(whole, axis=0)[None] - whole  43.5 us
    all_gather x1, blocking collectives, shared_solve(): collected = lax.all_gather(solved, 'sample', axis=0, tiled=True)  21.9 us
    dot_general x44, matrix products, inner_products(): lax.dot_general(left_cols, right_cols, (((0,), (0,)), ((), ())), preferre...  15.5 us
    reduce_sum x1, other arithmetic, weights_for(): rest_grams = jnp.sum(whole, axis=0)[None] - whole  12.1 us
  transfers between devices with their start and end apart: 1, of which 1 were waited for; matrix products, arithmetic and copies ran while one was open for 1% of the time, Pallas kernels for 0%

commit v1 on v0

v1 whole, which is shorter than its diff:
```python
import jax
import jax.numpy as jnp
from jax import lax
from jax.sharding import PartitionSpec as P

SNPS = 500
FOLDS = 5
PANEL = 128
HIGH = lax.Precision.HIGHEST


def standardize(genotype, allele_freq):
    spread = jnp.sqrt(2.0 * allele_freq * (1.0 - allele_freq))
    return ((genotype.astype(jnp.float32) - 2.0 * allele_freq) / spread).astype(jnp.bfloat16)


def predict(columns, weights):
    stacked = jnp.transpose(weights, (2, 0, 1)).reshape(-1, weights.shape[1])
    product = lax.dot_general(
        stacked, columns, (((1,), (1,)), ((), ())), preferred_element_type=jnp.float32
    )
    return product.astype(jnp.bfloat16).reshape(
        weights.shape[2], weights.shape[0], columns.shape[0]
    )


def inner_products(left_cols, right_cols):
    return lax.dot_general(
        left_cols, right_cols, (((0,), (0,)), ((), ())), preferred_element_type=jnp.float32
    )


def tile_pairs(panels):
    pairs = []
    for row_tile in range(panels):
        for col_tile in range(row_tile, panels):
            pairs.append((row_tile, col_tile))
    return pairs


def tile_grams(left_cols, right_cols, panels):
    tile_list = []
    for row_tile, col_tile in tile_pairs(panels):
        first = left_cols[:, row_tile * PANEL : (row_tile + 1) * PANEL]
        second = right_cols[:, col_tile * PANEL : (col_tile + 1) * PANEL]
        tile_list.append(inner_products(first, second))
    return jnp.stack(tile_list)


def mm(spec, left, right):
    return jnp.einsum(spec, left, right, precision=HIGH, preferred_element_type=jnp.float32)


def block_solve(tiles, target, panels):
    pairs = tile_pairs(panels)
    upper = {pair: tiles[:, index] for index, pair in enumerate(pairs)}
    eye = jnp.broadcast_to(jnp.eye(PANEL, dtype=jnp.float32), (tiles.shape[0], PANEL, PANEL))
    lower = {}
    inverse = {}
    for p in range(panels):
        factor = jnp.linalg.cholesky(upper[(p, p)])
        inv = lax.linalg.triangular_solve(factor, eye, left_side=True, lower=True)
        inverse[p] = inv
        for q in range(p + 1, panels):
            lower[(q, p)] = mm("sji,skj->sik", upper[(p, q)], inv)
        for r in range(p + 1, panels):
            for q in range(r, panels):
                upper[(r, q)] = upper[(r, q)] - mm("sik,sjk->sij", lower[(r, p)], lower[(q, p)])
    forward = []
    for p in range(panels):
        rhs = target[:, p * PANEL : (p + 1) * PANEL]
        for q in range(p):
            rhs = rhs - mm("sij,sjc->sic", lower[(p, q)], forward[q])
        forward.append(mm("sij,sjc->sic", inverse[p], rhs))
    backward = [None] * panels
    for p in reversed(range(panels)):
        rhs = forward[p]
        for q in range(p + 1, panels):
            rhs = rhs - mm("sji,sjc->sic", lower[(q, p)], backward[q])
        backward[p] = mm("sji,sjc->sic", inverse[p], rhs)
    return jnp.concatenate(backward, axis=1)


def shared_solve(summed_grams, summed_crosses, shrinkage, counts, panels):
    member_count = summed_grams.shape[1]
    ridge_count = shrinkage.shape[0]
    systems = FOLDS * member_count * ridge_count
    devices = lax.axis_size("sample")
    share = -(-systems // devices)
    owned_ids = lax.axis_index("sample") * share + lax.broadcasted_iota(jnp.int32, (share,), 0)
    owned_ids = jnp.minimum(owned_ids, systems - 1)
    pair_ids = owned_ids // ridge_count
    ridge_ids = owned_ids % ridge_count
    fold_ids = pair_ids // member_count
    member_ids = pair_ids % member_count
    fold_axis = jnp.arange(FOLDS, dtype=jnp.int32)[:, None, None]
    member_axis = jnp.arange(member_count, dtype=jnp.int32)[None, :, None]
    keep = jnp.logical_and(fold_axis != fold_ids[None, None, :], member_axis == member_ids[None, None, :])
    keep = keep.astype(jnp.float32)
    rest_tiles = jnp.einsum("kms,kmtij->stij", keep, summed_grams, precision=HIGH)
    rest_crosses = jnp.einsum("kms,kmic->sic", keep, summed_crosses, precision=HIGH)
    chosen_counts = jnp.take(counts, fold_ids, axis=0)
    ridge = jnp.take(shrinkage, ridge_ids, axis=0)
    width = rest_tiles.shape[-1]
    diag_ids = [index for index, (row_tile, col_tile) in enumerate(tile_pairs(panels)) if row_tile == col_tile]
    is_diag = jnp.zeros((len(tile_pairs(panels)),), jnp.float32).at[jnp.array(diag_ids)].set(1.0)
    position = lax.broadcasted_iota(jnp.int32, (panels, width), 1) + PANEL * lax.broadcasted_iota(
        jnp.int32, (panels, width), 0
    )
    padded = (position >= SNPS).astype(jnp.float32)
    pad_diag = jnp.zeros((len(tile_pairs(panels)), width), jnp.float32).at[jnp.array(diag_ids)].set(padded)
    identity = jnp.eye(width, dtype=jnp.float32)
    diag_add = (
        ridge[:, None, None] * is_diag[None, :, None]
        + (1.0 - ridge[:, None, None]) * pad_diag[None, :, :]
    )
    system = rest_tiles / chosen_counts[:, None, None, None] + diag_add[:, :, :, None] * identity
    target = rest_crosses / chosen_counts[:, None, None]
    solved = block_solve(system, target, panels)[:, :SNPS].astype(jnp.bfloat16)
    collected = lax.all_gather(solved, "sample", axis=0, tiled=True)
    return collected[:systems].reshape(FOLDS, member_count, ridge_count, SNPS, -1)


def shards(genotype, allele_freq, phenotype, shrinkage, owner_order):
    sample_rows = genotype.shape[0]
    total_rows = sample_rows * lax.axis_size("sample")
    scaled = standardize(genotype, allele_freq)
    ordered = jnp.take(phenotype, owner_order, axis=1)
    local_blocks = allele_freq.shape[0] // SNPS
    panels = -(-SNPS // PANEL)
    padded_width = panels * PANEL
    column_sets = [scaled[:, member * SNPS : (member + 1) * SNPS] for member in range(local_blocks)]
    bounds = [-(-(k * total_rows) // FOLDS) for k in range(FOLDS + 1)]
    counts = jnp.array(
        [float(total_rows - (bounds[k + 1] - bounds[k])) for k in range(FOLDS)], dtype=jnp.float32
    )
    start_row = lax.axis_index("sample") * sample_rows
    row_ids = start_row + lax.broadcasted_iota(jnp.int32, (sample_rows,), 0)
    fold_of = row_ids * FOLDS // total_rows
    first_fold = start_row * FOLDS // total_rows
    slot_folds = [first_fold, first_fold + 1]
    slot_masks = [fold_of == slot_folds[0], fold_of == slot_folds[1]]
    picked = jnp.minimum(jnp.stack(slot_folds), FOLDS - 1)
    fold_ids = jnp.arange(FOLDS, dtype=jnp.int32)
    tile_count = len(tile_pairs(panels))

    def fold_partials(member):
        columns = jnp.pad(column_sets[member], ((0, 0), (0, padded_width - SNPS)))
        gram_total = jnp.zeros((FOLDS, tile_count, PANEL, PANEL), jnp.float32)
        cross_total = jnp.zeros((FOLDS, padded_width, ordered.shape[1]), jnp.float32)
        for slot in range(2):
            masked = jnp.where(slot_masks[slot][:, None], columns, jnp.zeros_like(columns))
            selector = (fold_ids == slot_folds[slot]).astype(jnp.float32)
            gram_total = (
                gram_total
                + selector[:, None, None, None] * tile_grams(masked, columns, panels)[None]
            )
            cross_total = (
                cross_total + selector[:, None, None] * inner_products(masked, ordered)[None]
            )
        return (gram_total, cross_total)

    def weights_for(members):
        parts = [fold_partials(member) for member in members]
        grams = jnp.stack([item[0] for item in parts], axis=1)
        crosses = jnp.stack([item[1] for item in parts], axis=1)
        summed_grams, summed_crosses = lax.psum((grams, crosses), "sample")
        every_weights = shared_solve(summed_grams, summed_crosses, shrinkage, counts, panels)
        return jnp.take(every_weights, picked, axis=0)

    def fold_predictions(member, slot_weights):
        columns = column_sets[member]
        lower = predict(columns, slot_weights[0])
        upper = predict(columns, slot_weights[1])
        return jnp.where(slot_masks[1][None, None, :], upper, lower)

    weights = weights_for(list(range(local_blocks)))
    local_preds = jnp.concatenate(
        [fold_predictions(member, weights[:, member]) for member in range(local_blocks)], axis=1
    )
    return lax.all_to_all(local_preds, "block", split_axis=0, concat_axis=1, tiled=True)


def solution(mesh):
    in_specs = (P("sample", "block"), P("block"), P("sample", None), P(), P())
    out_specs = P("block", None, "sample")
    return jax.shard_map(shards, mesh=mesh, in_specs=in_specs, out_specs=out_specs, check_vma=False)
```

time: 606 us -> 518 us (0.85)
  other arithmetic: 316 us -> 205 us
  waiting for transfers between devices: 146 us -> 205 us
  local copies, waits for them, and re-layouts: 53.5 us -> 10.7 us
  matrix products: 37.2 us -> 46.8 us
    psum x1, waiting for transfers between devices: 146 us -> 205 us  [weights_for(): summed_grams, summed_crosses = lax.psum((grams, crosses), 'sample')]
    another operation x27 -> x22, other arithmetic: 237 us -> 182 us  [the longest x13 97.8 us: block_solve(): factor = jnp.linalg.cholesky(upper[p, p])]
    sub x2 -> x1, other arithmetic: 43.5 us -> 0.02 us  [shared_solve(): 1.0 - ridge[:, None, None]]
    dot_general x0 -> x38, matrix products: none -> 32.2 us  [the longest x36 20.4 us: mm(): jnp.einsum(spec, left, right, precision=HIGH, preferred_element_type=jnp....]
    another operation x20 -> x4, matrix products: 20.3 us -> 2.45 us  [block_solve(): inv = lax.linalg.triangular_solve(factor, eye, left_side=True, lower=True)]
    reduce_sum x2 -> x0, other arithmetic: 12.1 us -> none  [the longest x1 12.1 us: weights_for(): rest_grams = jnp.sum(whole, axis=0)[None] - whole]
    another operation x20 -> x0, local copies, waits for them, and re-layouts: 11.2 us -> none
    unnamed x68 -> x34, local copies, waits for them, and re-layouts: 10.8 us -> 0.07 us
where the time goes in v1:
time: 518 us; the launch traced here: 511 us
  other arithmetic  205 us (40%)
  waiting for transfers between devices  205 us (40%)
  matrix products  46.8 us (9%)
  blocking collectives  28.9 us (6%)
  between operations  14.7 us (3%)
  local copies, waits for them, and re-layouts  10.7 us (2%)
    psum x1, waiting for transfers between devices, weights_for(): summed_grams, summed_crosses = lax.psum((grams, crosses), 'sample')  205 us
    another operation x13, other arithmetic, block_solve(): factor = jnp.linalg.cholesky(upper[p, p])  97.8 us
    another operation x9, other arithmetic, block_solve(): inv = lax.linalg.triangular_solve(factor, eye, left_side=True, lower=True)  83.8 us
    all_gather x1, blocking collectives, shared_solve(): collected = lax.all_gather(solved, 'sample', axis=0, tiled=True)  21.9 us
    dot_general x36, matrix products, mm(): jnp.einsum(spec, left, right, precision=HIGH, preferred_element_type=jnp....  20.4 us
    dot_general x44, matrix products, inner_products(): lax.dot_general(left_cols, right_cols, (((0,), (0,)), ((), ())), preferre...  10.8 us
  transfers between devices with their start and end apart: 1, of which 1 were waited for; matrix products, arithmetic and copies ran while one was open for 1% of the time, Pallas kernels for 0%

profile of v1, /device:TPU:0, one launch (start us, length us, event | category | flops | bytes accessed | tf_op | source)
XLA Modules:
  0.0 510.9 jit_solution(4476587535390059192)
XLA Ops:
  8.6 2.7 divide_convert_fusion
  25.3 1.4 multiply_add_fusion.1
  26.7 4.9 pad_maximum_fusion
  33.7 1.2 scatter_custom_fusion
  37.8 205.0 %all-reduce.4.cloned.1.call-done = (f32[5,2,10,128,128]{4,0,1,3,2:T(8,128)}, f32[5,2,512,16]{2,0,1,3:T(8,128)}) async-done(((f32[5,2,10,128,128]{4,0,1,3,2:T(8,128)}, f32[5,2,512,16]{2,0,1,3:T(8,128)}), (f32[5,2,10,128,128]{4,0,1,3,2:T(8,128)}, f32[5,2,512,16]{2,0,1,3:T(8,128)})) %all-reduce.4.cloned.1.call-update) | async-done | bytes 6881296 | tf_op jit(solution)/shard_map/psum | solution.py:167
  242.8 10.3 %convolution_bitcast_fusion = f32[2,10,128,128]{3,0,2,1:T(2,128)S(1)} fusion(f32[5,2,10,128,128]{4,0,1,3,2:T(8,128)} %get-tuple-element.6, pred[2,2]{1,0:T(4,128)(4,1)S(1)} %iota_compare_fusion.3, pred[5,2]{0,1:T(4,128)(4,1)S(1)} %iota_compare_fusion.4), kind=kOutput, calls=%fused_computation.9 | convolution fusion | flops 39321620 | bytes 7864334 | tf_op jit(solution)/shard_map/kms,kmtij->stij/dot_general | solution.py:100
  253.1 2.5 copy.154
  255.7 1.7 multiply_add_fusion.2
  258.1 1.7 copy.155
  259.8 1.6 fusion.97
  261.3 24.9 %custom-call.12 = f32[2,128,128]{2,1,0:T(8,128)} custom-call(f32[2,128,128]{2,1,0:T(8,128)} %fusion.97), custom_call_target="Cholesky" | custom-call | tf_op jit(solution)/shard_map/jit(cholesky)/cholesky | solution.py:61
  287.3 1.6 select_bitcast_fusion.3
  288.9 21.1 %custom-call.13 = f32[2,1,128,128]{2,3,1,0:T(8,128)} custom-call(f32[2,1,128,128]{3,2,1,0:T(8,128)} %select_bitcast_fusion.3), custom_call_target="InvertDiagBlocksLowerTriangular" | custom-call | tf_op jit(solution)/shard_map/triangular_solve/custom-call.0 | solution.py:62
  310.0 1.3 fusion.107
  311.7 1.4 fusion.95
  313.1 1.3 fusion.96
  314.4 1.5 convolution_bitcast_fusion.1
  317.0 1.3 convolution_subtract_fusion.9
  320.7 1.1 convolution_subtract_fusion.5
  322.7 23.7 %custom-call.14 = f32[2,128,128]{2,1,0:T(8,128)S(1)} custom-call(f32[2,128,128]{2,1,0:T(8,128)S(1)} %fusion.106), custom_call_target="Cholesky" | custom-call | tf_op jit(solution)/shard_map/jit(cholesky)/cholesky | solution.py:61
  346.6 19.7 %custom-call.15 = f32[2,1,128,128]{2,3,1,0:T(8,128)S(1)} custom-call(f32[2,1,128,128]{3,2,1,0:T(8,128)S(1)} %select_bitcast_fusion.2), custom_call_target="InvertDiagBlocksLowerTriangular" | custom-call | tf_op jit(solution)/shard_map/triangular_solve/custom-call.0 | solution.py:62
  369.8 1.3 convolution_subtract_fusion.3
  371.5 1.1 convolution_subtract_fusion.1
  372.7 23.5 %custom-call.16 = f32[2,128,128]{2,1,0:T(8,128)S(1)} custom-call(f32[2,128,128]{2,1,0:T(8,128)S(1)} %fusion.103), custom_call_target="Cholesky" | custom-call | tf_op jit(solution)/shard_map/jit(cholesky)/cholesky | solution.py:61
  396.4 19.9 %custom-call.17 = f32[2,1,128,128]{2,3,1,0:T(8,128)S(1)} custom-call(f32[2,1,128,128]{3,2,1,0:T(8,128)S(1)} %select_bitcast_fusion.1), custom_call_target="InvertDiagBlocksLowerTriangular" | custom-call | tf_op jit(solution)/shard_map/triangular_solve/custom-call.0 | solution.py:62
  417.4 1.3 convolution_subtract_fusion
  419.5 1.6 fusion.100
  421.1 24.3 %custom-call.18 = f32[2,128,128]{2,1,0:T(8,128)S(1)} custom-call(f32[2,128,128]{2,1,0:T(8,128)} %fusion.100), custom_call_target="Cholesky" | custom-call | tf_op jit(solution)/shard_map/jit(cholesky)/cholesky | solution.py:61
  446.3 20.5 %custom-call.19 = f32[2,1,128,128]{2,3,1,0:T(8,128)S(1)} custom-call(f32[2,1,128,128]{3,2,1,0:T(8,128)} %select_bitcast_fusion), custom_call_target="InvertDiagBlocksLowerTriangular" | custom-call | tf_op jit(solution)/shard_map/triangular_solve/custom-call.0 | solution.py:62
  467.1 1.0 convolution_subtract_fusion.16
  470.9 21.9 %all_gather.3 = bf16[32,500,16]{1,2,0:T(8,128)(2,1)S(1)} all-gather(bf16[2,500,16]{1,2,0:T(8,128)(2,1)S(1)} %pad_maximum_fusion.3), channel_id=1, replica_groups=mesh['sample'=16,'block'=2] {'sample'}, dimensions={0}, use_global_device_ids=true | all-gather | bytes 544000 | tf_op jit(solution)/shard_map/all_gather | solution.py:120
  495.8 7.0 %all_to_all.18 = bf16[16,4,1024]{2,1,0:T(4,128)(2,1)S(1)} all-to-all(bf16[16,4,1024]{2,1,0:T(4,128)(2,1)S(1)} %pad_maximum_fusion.2), channel_id=1, replica_groups=mesh['sample'=16,'block'=2] {'block'}, dimensions={0} | all-to-all | bytes 262144 | tf_op jit(solution)/shard_map/all_to_all | solution.py:181
  (185 shorter events, 40.9 us)
Async XLA Ops:
  6.5 5.1 copy-start
  6.5 236.2 %all-reduce.4.cloned.1.call-start = ((), (), s32[]{:S(2)}) async-start(), calls=%async_computation.1 | async-start | bytes 22020096 | tf_op jit(solution)/shard_map/psum | solution.py:167
  7.9 5.1 copy-start.10
  12.2 0.8 copy-start.15
  31.6 0.8 copy-start.2
  31.6 1.5 copy-start.1
  31.6 5.4 %copy-start.16 = (f32[10]{0:T(128)S(1)}, f32[10]{0:T(128)}, u32[]{:S(2)}) copy-start(f32[10]{0:T(128)} %constant.196) | copy-start | bytes 124
  31.7 211.1 %copy-start.9 = (f32[128,128]{0,1:T(8,128)}, f32[128,128]{0,1:T(8,128)S(1)}, u32[]{:S(2)}) copy-start(f32[128,128]{0,1:T(8,128)S(1)} %fusion.125) | copy-start | bytes 196612
  36.3 216.8 %copy-start.12 = (pred[2,2]{1,0:T(4,128)(4,1)}, pred[2,2]{1,0:T(4,128)(4,1)S(1)}, u32[]{:S(2)}) copy-start(pred[2,2]{1,0:T(4,128)(4,1)S(1)} %iota_compare_fusion.3) | copy-start | bytes 16
  36.4 216.7 %copy-start.13 = (pred[5,2]{0,1:T(4,128)(4,1)}, pred[5,2]{0,1:T(4,128)(4,1)S(1)}, u32[]{:S(2)}) copy-start(pred[5,2]{0,1:T(4,128)(4,1)S(1)} %iota_compare_fusion.4) | copy-start | bytes 34
  255.7 54.3 %copy-start.7 = (f32[128,128]{1,0:T(8,128)S(1)}, f32[128,128]{1,0:T(8,128)}, u32[]{:S(2)}) copy-start(f32[128,128]{1,0:T(8,128)} %copy.156) | copy-start | bytes 196612
  257.4 53.9 %copy-start.3 = (f32[2,10,128,128]{2,3,0,1:T(8,128)}, f32[2,10,128,128]{2,3,0,1:T(8,128)S(1)}, u32[]{:S(2)}) copy-start(f32[2,10,128,128]{2,3,0,1:T(8,128)S(1)} %multiply_add_fusion.2) | copy-start | bytes 3932164
  311.3 9.4 %copy-start.5 = (f32[2,128,128]{2,1,0:T(8,128)}, f32[2,128,128]{2,1,0:T(8,128)S(1)}, u32[]{:S(2)}) copy-start(f32[2,128,128]{2,1,0:T(8,128)S(1)} %fusion.107) | copy-start | bytes 393220
  311.7 7.3 %copy-start.4 = (f32[2,10,128,128]{2,3,0,1:T(8,128)S(1)}, f32[2,10,128,128]{2,3,0,1:T(8,128)}, u32[]{:S(2)}) copy-start(f32[2,10,128,128]{2,3,0,1:T(8,128)} %copy-done.3) | copy-start | bytes 3932164
  318.7 47.7 %copy-start.8 = (f32[128,128]{1,0:T(8,128)S(1)}, f32[128,128]{1,0:T(8,128)}, u32[]{:S(2)}) copy-start(f32[128,128]{1,0:T(8,128)} %copy.156) | copy-start | bytes 196612
  417.1 53.5 %copy-start.6 = (f32[2,128,128]{2,1,0:T(8,128)S(1)}, f32[2,128,128]{2,1,0:T(8,128)}, u32[]{:S(2)}) copy-start(f32[2,128,128]{2,1,0:T(8,128)} %copy-done.5) | copy-start | bytes 393220
  469.9 23.6 %copy-start.14 = (pred[2]{0:T(512)(128)(4,1)S(1)}, pred[2]{0:T(512)(128)(4,1)}, u32[]{:S(2)}) copy-start(pred[2]{0:T(512)(128)(4,1)} %compare_and_fusion.1) | copy-start | bytes 10
  494.7 0.9 copy-start.11
Sparse Core Ops, SparseCore 0:
  31.8 210.9 all-reduce.3

commit v2 on v1

v2 whole, which is shorter than its diff:
```python
import jax
import jax.numpy as jnp
from jax import lax
from jax.sharding import PartitionSpec as P

SNPS = 500
FOLDS = 5
PANEL = 128
HIGH = lax.Precision.HIGHEST


def standardize(genotype, allele_freq):
    spread = jnp.sqrt(2.0 * allele_freq * (1.0 - allele_freq))
    return ((genotype.astype(jnp.float32) - 2.0 * allele_freq) / spread).astype(jnp.bfloat16)


def predict(columns, weights):
    stacked = jnp.transpose(weights, (2, 0, 1)).reshape(-1, weights.shape[1])
    product = lax.dot_general(
        stacked, columns, (((1,), (1,)), ((), ())), preferred_element_type=jnp.float32
    )
    return product.astype(jnp.bfloat16).reshape(
        weights.shape[2], weights.shape[0], columns.shape[0]
    )


def inner_products(left_cols, right_cols):
    return lax.dot_general(
        left_cols, right_cols, (((0,), (0,)), ((), ())), preferred_element_type=jnp.float32
    )


def tile_pairs(panels):
    pairs = []
    for row_tile in range(panels):
        for col_tile in range(row_tile, panels):
            pairs.append((row_tile, col_tile))
    return pairs


def tile_grams(left_cols, right_cols, panels):
    tile_list = []
    for row_tile, col_tile in tile_pairs(panels):
        first = left_cols[:, row_tile * PANEL : (row_tile + 1) * PANEL]
        second = right_cols[:, col_tile * PANEL : (col_tile + 1) * PANEL]
        tile_list.append(inner_products(first, second))
    return jnp.stack(tile_list)


def mm(spec, left, right):
    return jnp.einsum(spec, left, right, precision=HIGH, preferred_element_type=jnp.float32)


def block_solve(tiles, target, panels):
    pairs = tile_pairs(panels)
    upper = {pair: tiles[:, index] for index, pair in enumerate(pairs)}
    eye = jnp.broadcast_to(jnp.eye(PANEL, dtype=jnp.float32), (tiles.shape[0], PANEL, PANEL))
    lower = {}
    inverse = {}
    for p in range(panels):
        factor = jnp.linalg.cholesky(upper[(p, p)])
        inv = lax.linalg.triangular_solve(factor, eye, left_side=True, lower=True)
        inverse[p] = inv
        for q in range(p + 1, panels):
            lower[(q, p)] = mm("sji,skj->sik", upper[(p, q)], inv)
        for r in range(p + 1, panels):
            for q in range(r, panels):
                upper[(r, q)] = upper[(r, q)] - mm("sik,sjk->sij", lower[(r, p)], lower[(q, p)])
    forward = []
    for p in range(panels):
        rhs = target[:, p * PANEL : (p + 1) * PANEL]
        for q in range(p):
            rhs = rhs - mm("sij,sjc->sic", lower[(p, q)], forward[q])
        forward.append(mm("sij,sjc->sic", inverse[p], rhs))
    backward = [None] * panels
    for p in reversed(range(panels)):
        rhs = forward[p]
        for q in range(p + 1, panels):
            rhs = rhs - mm("sji,sjc->sic", lower[(q, p)], backward[q])
        backward[p] = mm("sji,sjc->sic", inverse[p], rhs)
    return jnp.concatenate(backward, axis=1)


def owned_layout(systems, devices, ridge_count):
    share = -(-systems // devices)
    firsts = []
    spans = []
    for device in range(devices):
        first = min(device * share, systems - 1) // ridge_count
        last = min(device * share + share - 1, systems - 1) // ridge_count
        firsts.append(first)
        spans.append(last - first + 1)
    return share, firsts, max(spans)


def shards(genotype, allele_freq, phenotype, shrinkage, owner_order):
    sample_rows = genotype.shape[0]
    devices = lax.axis_size("sample")
    me = lax.axis_index("sample")
    total_rows = sample_rows * devices
    scaled = standardize(genotype, allele_freq)
    ordered = jnp.take(phenotype, owner_order, axis=1)
    traits = ordered.shape[1]
    member_count = allele_freq.shape[0] // SNPS
    ridge_count = shrinkage.shape[0]
    panels = -(-SNPS // PANEL)
    padded_width = panels * PANEL
    tile_count = len(tile_pairs(panels))
    pair_count = FOLDS * member_count
    systems = pair_count * ridge_count
    share, firsts, span = owned_layout(systems, devices, ridge_count)
    column_sets = [scaled[:, member * SNPS : (member + 1) * SNPS] for member in range(member_count)]
    bounds = [-(-(k * total_rows) // FOLDS) for k in range(FOLDS + 1)]
    counts = jnp.array(
        [float(total_rows - (bounds[k + 1] - bounds[k])) for k in range(FOLDS)], dtype=jnp.float32
    )
    start_row = me * sample_rows
    row_ids = start_row + lax.broadcasted_iota(jnp.int32, (sample_rows,), 0)
    fold_of = row_ids * FOLDS // total_rows
    first_fold = start_row * FOLDS // total_rows
    slot_folds = [first_fold, first_fold + 1]
    slot_masks = [fold_of == slot_folds[0], fold_of == slot_folds[1]]
    picked = jnp.minimum(jnp.stack(slot_folds), FOLDS - 1)

    gram_parts = []
    cross_parts = []
    for member in range(member_count):
        columns = jnp.pad(column_sets[member], ((0, 0), (0, padded_width - SNPS)))
        slot_grams = []
        slot_crosses = []
        for slot in range(2):
            masked = jnp.where(slot_masks[slot][:, None], columns, jnp.zeros_like(columns))
            slot_grams.append(tile_grams(masked, columns, panels))
            slot_crosses.append(inner_products(masked, ordered))
        gram_parts.append(jnp.stack(slot_grams))
        cross_parts.append(jnp.stack(slot_crosses))
    local_grams = jnp.stack(gram_parts, axis=1)
    local_crosses = jnp.stack(cross_parts, axis=1)

    wanted = []
    for device in range(devices):
        for offset in range(span):
            wanted.append(min(firsts[device] + offset, pair_count - 1))
    wanted_folds = jnp.array([pair // member_count for pair in wanted], jnp.int32)
    wanted_members = jnp.array([pair % member_count for pair in wanted], jnp.int32)
    member_axis = jnp.arange(member_count, dtype=jnp.int32)
    coefficient = jnp.stack(
        [
            jnp.logical_and(wanted_folds[:, None] != slot_folds[slot], wanted_members[:, None] == member_axis[None, :])
            for slot in range(2)
        ],
        axis=1,
    ).astype(jnp.float32)
    gram_payload = jnp.einsum("wjm,jmtab->wtab", coefficient, local_grams, precision=HIGH)
    cross_payload = jnp.einsum("wjm,jmic->wic", coefficient, local_crosses, precision=HIGH)
    gram_rows = gram_payload.reshape(devices, span * tile_count * PANEL, PANEL)
    cross_rows = cross_payload.reshape(devices, span * padded_width * traits // PANEL, PANEL)
    payload = jnp.concatenate([gram_rows, cross_rows], axis=1)
    reduced = lax.psum_scatter(payload, "sample", scatter_dimension=0, tiled=True)[0]
    split = span * tile_count * PANEL
    mine_grams = reduced[:split].reshape(span, tile_count, PANEL, PANEL)
    mine_crosses = reduced[split:].reshape(span, padded_width, traits)

    owned_ids = jnp.minimum(me * share + lax.broadcasted_iota(jnp.int32, (share,), 0), systems - 1)
    pair_ids = owned_ids // ridge_count
    ridge_ids = owned_ids % ridge_count
    local_ids = pair_ids - jnp.take(jnp.array(firsts, jnp.int32), me)
    rest_tiles = jnp.take(mine_grams, local_ids, axis=0)
    rest_crosses = jnp.take(mine_crosses, local_ids, axis=0)
    chosen_counts = jnp.take(counts, pair_ids // member_count, axis=0)
    ridge = jnp.take(shrinkage, ridge_ids, axis=0)
    diag_ids = [index for index, (row_tile, col_tile) in enumerate(tile_pairs(panels)) if row_tile == col_tile]
    is_diag = jnp.zeros((tile_count,), jnp.float32).at[jnp.array(diag_ids)].set(1.0)
    position = lax.broadcasted_iota(jnp.int32, (panels, PANEL), 1) + PANEL * lax.broadcasted_iota(
        jnp.int32, (panels, PANEL), 0
    )
    padded = (position >= SNPS).astype(jnp.float32)
    pad_diag = jnp.zeros((tile_count, PANEL), jnp.float32).at[jnp.array(diag_ids)].set(padded)
    identity = jnp.eye(PANEL, dtype=jnp.float32)
    diag_add = (
        ridge[:, None, None] * is_diag[None, :, None]
        + (1.0 - ridge[:, None, None]) * pad_diag[None, :, :]
    )
    system = rest_tiles / chosen_counts[:, None, None, None] + diag_add[:, :, :, None] * identity
    target = rest_crosses / chosen_counts[:, None, None]
    solved = block_solve(system, target, panels)[:, :SNPS].astype(jnp.bfloat16)
    collected = lax.all_gather(solved, "sample", axis=0, tiled=True)
    every_weights = collected[:systems].reshape(FOLDS, member_count, ridge_count, SNPS, traits)
    weights = jnp.take(every_weights, picked, axis=0)

    def fold_predictions(member, slot_weights):
        columns = column_sets[member]
        lower = predict(columns, slot_weights[0])
        upper = predict(columns, slot_weights[1])
        return jnp.where(slot_masks[1][None, None, :], upper, lower)

    local_preds = jnp.concatenate(
        [fold_predictions(member, weights[:, member]) for member in range(member_count)], axis=1
    )
    return lax.all_to_all(local_preds, "block", split_axis=0, concat_axis=1, tiled=True)


def solution(mesh):
    in_specs = (P("sample", "block"), P("block"), P("sample", None), P(), P())
    out_specs = P("block", None, "sample")
    return jax.shard_map(shards, mesh=mesh, in_specs=in_specs, out_specs=out_specs, check_vma=False)
```

time: 518 us -> 456 us (0.88)
  waiting for transfers between devices: 205 us -> 119 us
  local copies, waits for them, and re-layouts: 10.7 us -> 28.5 us
  matrix products: 46.8 us -> 53.7 us
    psum x1 -> x0, waiting for transfers between devices: 205 us -> none  [weights_for(): summed_grams, summed_crosses = lax.psum((grams, crosses), 'sample')]
    reduce_scatter x0 -> x1, waiting for transfers between devices: none -> 119 us  [shards(): lax.psum_scatter(payload, 'sample', scatter_dimension=0, tiled=True)[0]]
    reshape x0 -> x2, local copies, waits for them, and re-layouts: none -> 11.6 us  [the longest x1 7.46 us: shards(): gram_rows = gram_payload.reshape(devices, span * tile_count * PANEL, PANEL)]
    concatenate x0 -> x1, other arithmetic: none -> 9.23 us  [shards(): payload = jnp.concatenate([gram_rows, cross_rows], axis=1)]
    dot_general x36, matrix products: 20.4 us -> 26.5 us  [mm(): jnp.einsum(spec, left, right, precision=HIGH, preferred_element_type=jnp....]
    another operation x2 -> x6, other arithmetic: 5.75 us -> 0.38 us  [the longest x3 0.36 us: shards(): local_grams = jnp.stack(gram_parts, axis=1)]
where the time goes in v2:
time: 456 us; the launch traced here: 451 us
  other arithmetic  206 us (45%)
  waiting for transfers between devices  119 us (26%)
  matrix products  53.7 us (12%)
  local copies, waits for them, and re-layouts  28.5 us (6%)
  blocking collectives  28.2 us (6%)
  between operations  15.4 us (3%)
    reduce_scatter x1, waiting for transfers between devices, shards(): lax.psum_scatter(payload, 'sample', scatter_dimension=0, tiled=True)[0]  119 us
    another operation x13, other arithmetic, block_solve(): factor = jnp.linalg.cholesky(upper[p, p])  97.8 us
    another operation x9, other arithmetic, block_solve(): inv = lax.linalg.triangular_solve(factor, eye, left_side=True, lower=True)  83.7 us
    dot_general x36, matrix products, mm(): jnp.einsum(spec, left, right, precision=HIGH, preferred_element_type=jnp....  26.5 us
    all_gather x1, blocking collectives, shards(): collected = lax.all_gather(solved, 'sample', axis=0, tiled=True)  21.2 us
    dot_general x44, matrix products, inner_products(): lax.dot_general(left_cols, right_cols, (((0,), (0,)), ((), ())), preferre...  14.2 us
    concatenate x1, other arithmetic, shards(): payload = jnp.concatenate([gram_rows, cross_rows], axis=1)  9.23 us
  transfers between devices with their start and end apart: 1, of which 1 were waited for; matrix products, arithmetic and copies ran while one was open for 1% of the time, Pallas kernels for 0%

profile of v2, /device:TPU:0, one launch (start us, length us, event | category | flops | bytes accessed | tf_op | source)
XLA Modules:
  0.0 451.4 jit_solution(3329636785308102021)
XLA Ops:
  8.6 2.7 divide_convert_fusion
  13.0 2.3 slice_select_fusion
  19.3 3.5 copy.115
  22.8 4.1 reshape.583
  40.0 7.9 %fusion = f32[16,10,128,128,1]{3,0,4,2,1:T(8,128)S(1)} fusion(f32[2,2,10,128,128]{4,3,2,0,1:T(8,128)S(1)} %pad_maximum_fusion.1, pred[16,1,2]{0,2,1:T(4,128)(4,1)S(1)} %get-tuple-element.45, pred[16,1,2]{0,2,1:T(4,128)(4,1)S(1)} %get-tuple-element.44), kind=kOutput, calls=%fused_computation.8 | convolution fusion | flops 125829184 | bytes 13107264 | tf_op jit(solution)/shard_map/wjm,jmtab->wtab/dot_general | solution.py:154
  47.9 7.5 %copy.116 = f32[16,1280,128]{2,1,0:T(8,128)} copy(f32[16,1280,128]{2,0,1:T(8,128)S(1)} %bitcast.375) | data formatting | bytes 20971520 | tf_op jit(solution)/shard_map/reshape | solution.py:156
  55.4 9.2 %pad_maximum_fusion = f32[16,1344,128]{2,1,0:T(8,128)} fusion(f32[16,64,128]{2,1,0:T(8,128)S(1)} %copy-done.13, f32[16,1280,128]{2,1,0:T(8,128)} %copy.116), kind=kLoop, calls=%fused_computation.5 | loop fusion | flops 2752512 | bytes 22020096 | tf_op jit(solution)/shard_map/concatenate | solution.py:158
  71.5 119.4 %reduce-scatter.2.cloned.1.call-done = f32[1,1344,128]{2,1,0:T(8,128)} async-done(((f32[16,1344,128]{2,1,0:T(8,128)}), f32[1,1344,128]{2,1,0:T(8,128)}) %reduce-scatter.2.cloned.1.call-update) | async-done | bytes 688144 | tf_op jit(solution)/shard_map/reduce_scatter | solution.py:159
  193.2 1.4 multiply_add_fusion
  195.3 1.7 copy.118
  197.0 1.6 fusion.99
  198.5 24.9 %custom-call.12 = f32[2,128,128]{2,1,0:T(8,128)} custom-call(f32[2,128,128]{2,1,0:T(8,128)} %fusion.99), custom_call_target="Cholesky" | custom-call | tf_op jit(solution)/shard_map/jit(cholesky)/cholesky | solution.py:61
  224.5 1.6 select_bitcast_fusion.3
  226.1 21.1 %custom-call.13 = f32[2,1,128,128]{2,3,1,0:T(8,128)} custom-call(f32[2,1,128,128]{3,2,1,0:T(8,128)} %select_bitcast_fusion.3), custom_call_target="InvertDiagBlocksLowerTriangular" | custom-call | tf_op jit(solution)/shard_map/triangular_solve/custom-call.0 | solution.py:62
  249.0 1.3 fusion.98
  251.6 1.3 convolution_subtract_fusion.4
  252.9 1.3 convolution_subtract_fusion.9
  255.5 2.0 convolution_subtract_fusion.5
  257.5 1.3 convolution_subtract_fusion.8
  258.8 2.0 convolution_subtract_fusion.7
  265.2 23.6 %custom-call.14 = f32[2,128,128]{2,1,0:T(8,128)S(1)} custom-call(f32[2,128,128]{2,1,0:T(8,128)S(1)} %fusion.108), custom_call_target="Cholesky" | custom-call | tf_op jit(solution)/shard_map/jit(cholesky)/cholesky | solution.py:61
  289.1 19.7 %custom-call.15 = f32[2,1,128,128]{2,3,1,0:T(8,128)S(1)} custom-call(f32[2,1,128,128]{3,2,1,0:T(8,128)S(1)} %select_bitcast_fusion.2), custom_call_target="InvertDiagBlocksLowerTriangular" | custom-call | tf_op jit(solution)/shard_map/triangular_solve/custom-call.0 | solution.py:62
  311.0 1.3 convolution_subtract_fusion.3
  312.3 1.3 convolution_subtract_fusion.6
  313.8 23.5 %custom-call.16 = f32[2,128,128]{2,1,0:T(8,128)S(1)} custom-call(f32[2,128,128]{2,1,0:T(8,128)S(1)} %fusion.105), custom_call_target="Cholesky" | custom-call | tf_op jit(solution)/shard_map/jit(cholesky)/cholesky | solution.py:61
  337.5 19.9 %custom-call.17 = f32[2,1,128,128]{2,3,1,0:T(8,128)S(1)} custom-call(f32[2,1,128,128]{3,2,1,0:T(8,128)S(1)} %select_bitcast_fusion.1), custom_call_target="InvertDiagBlocksLowerTriangular" | custom-call | tf_op jit(solution)/shard_map/triangular_solve/custom-call.0 | solution.py:62
  358.2 1.3 convolution_subtract_fusion
  360.2 1.6 fusion.102
  361.8 24.3 %custom-call.18 = f32[2,128,128]{2,1,0:T(8,128)S(1)} custom-call(f32[2,128,128]{2,1,0:T(8,128)} %fusion.102), custom_call_target="Cholesky" | custom-call | tf_op jit(solution)/shard_map/jit(cholesky)/cholesky | solution.py:61
  387.0 20.5 %custom-call.19 = f32[2,1,128,128]{2,3,1,0:T(8,128)S(1)} custom-call(f32[2,1,128,128]{3,2,1,0:T(8,128)} %select_bitcast_fusion), custom_call_target="InvertDiagBlocksLowerTriangular" | custom-call | tf_op jit(solution)/shard_map/triangular_solve/custom-call.0 | solution.py:62
  412.2 21.2 %all_gather.3 = bf16[32,500,16]{1,2,0:T(8,128)(2,1)S(1)} all-gather(bf16[2,500,16]{1,2,0:T(8,128)(2,1)S(1)} %pad_maximum_fusion.4), channel_id=1, replica_groups=mesh['sample'=16,'block'=2] {'sample'}, dimensions={0}, use_global_device_ids=true | all-gather | bytes 544000 | tf_op jit(solution)/shard_map/all_gather | solution.py:187
  436.5 7.0 %all_to_all.18 = bf16[16,4,1024]{2,1,0:T(4,128)(2,1)S(1)} all-to-all(bf16[16,4,1024]{2,1,0:T(4,128)(2,1)S(1)} %pad_maximum_fusion.3), channel_id=1, replica_groups=mesh['sample'=16,'block'=2] {'block'}, dimensions={0} | all-to-all | bytes 262144 | tf_op jit(solution)/shard_map/all_to_all | solution.py:200
  (234 shorter events, 52.8 us)
Async XLA Ops:
  6.5 5.0 %copy-start = (bf16[1024,16]{0,1:T(8,128)(2,1)S(1)}, bf16[1024,16]{0,1:T(8,128)(2,1)}, u32[]{:S(2)}) copy-start(bf16[1024,16]{0,1:T(8,128)(2,1)} %param.16) | copy-start | bytes 98308
  6.5 184.4 %reduce-scatter.2.cloned.1.call-start = ((), (), s32[]{:S(2)}) async-start(), calls=%async_computation.2 | async-start | bytes 11698176 | tf_op jit(solution)/shard_map/reduce_scatter | solution.py:159
  12.2 3.1 copy-start.24
  15.3 2.7 copy-start.7
  15.3 2.7 copy-start.9
  15.3 2.7 copy-start.16
  15.3 2.6 copy-start.34
  15.3 2.7 copy-start.33
  26.9 2.5 copy-start.12
  33.6 1.5 copy-start.17
  33.6 1.7 copy-start.19
  36.0 1.4 copy-start.8
  47.9 7.5 %copy-start.13 = (f32[16,64,128]{2,1,0:T(8,128)S(1)}, f32[16,64,128]{2,1,0:T(8,128)}, u32[]{:S(2)}) copy-start(f32[16,64,128]{2,1,0:T(8,128)} %reshape.583) | copy-start | bytes 1572868
  64.6 2.1 copy-start.2
  64.6 2.7 copy-start.3
  64.6 6.7 %copy-start.32 = (f32[10]{0:T(128)S(1)}, f32[10]{0:T(128)}, u32[]{:S(2)}) copy-start(f32[10]{0:T(128)} %constant.261) | copy-start | bytes 124
  65.9 5.6 %copy-start.20 = (f32[128,128]{0,1:T(8,128)}, f32[128,128]{0,1:T(8,128)S(1)}, u32[]{:S(2)}) copy-start(f32[128,128]{0,1:T(8,128)S(1)} %fusion.128) | copy-start | bytes 196612
  69.4 125.2 %copy-start.26 = (pred[2]{0:T(512)(128)(4,1)}, pred[2]{0:T(512)(128)(4,1)S(1)}, u32[]{:S(2)}) copy-start(pred[2]{0:T(512)(128)(4,1)S(1)} %compare_and_fusion.1) | copy-start | bytes 10
  71.5 121.7 %copy-start.28 = (f32[2]{0:T(128)S(1)}, f32[2]{0:T(128)}, u32[]{:S(2)}) copy-start(f32[2]{0:T(128)} %and_select_fusion.4) | copy-start | bytes 28
  193.2 54.0 %copy-start.14 = (f32[128,128]{1,0:T(8,128)S(1)}, f32[128,128]{1,0:T(8,128)}, u32[]{:S(2)}) copy-start(f32[128,128]{1,0:T(8,128)} %copy.119) | copy-start | bytes 196612
  194.6 54.0 %copy-start.4 = (f32[2,10,128,128]{2,3,0,1:T(8,128)}, f32[2,10,128,128]{2,3,0,1:T(8,128)S(1)}, u32[]{:S(2)}) copy-start(f32[2,10,128,128]{2,3,0,1:T(8,128)S(1)} %multiply_add_fusion) | copy-start | bytes 3932164
  248.5 12.2 %copy-start.5 = (f32[2,128,128]{2,1,0:T(8,128)}, f32[2,128,128]{2,1,0:T(8,128)S(1)}, u32[]{:S(2)}) copy-start(f32[2,128,128]{2,1,0:T(8,128)S(1)} %fusion.109) | copy-start | bytes 393220
  249.0 11.8 %slice-start = ((f32[1,1344,128]{2,1,0:T(8,128)}), f32[1,64,128]{2,1,0:T(8,128)S(1)}, s32[]{:S(2)}) async-start(f32[1,1344,128]{2,1,0:T(8,128)} %reduce-scatter.2.cloned.1.call-done), calls=%async_computation.3 | async-start | bytes 65536 | tf_op jit(solution)/shard_map/slice | solution.py:162
  250.3 10.7 %copy-start.27 = (pred[2]{0:T(512)(128)(4,1)S(1)}, pred[2]{0:T(512)(128)(4,1)}, u32[]{:S(2)}) copy-start(pred[2]{0:T(512)(128)(4,1)} %copy-done.26) | copy-start | bytes 10
  250.3 10.7 %copy-start.29 = (f32[2]{0:T(128)S(1)}, f32[2]{0:T(128)}, u32[]{:S(2)}) copy-start(f32[2]{0:T(128)} %and_select_fusion.4) | copy-start | bytes 28
  255.5 53.3 %copy-start.15 = (f32[128,128]{1,0:T(8,128)S(1)}, f32[128,128]{1,0:T(8,128)}, u32[]{:S(2)}) copy-start(f32[128,128]{1,0:T(8,128)} %copy.119) | copy-start | bytes 196612
  312.3 95.6 %copy-start.21 = (f32[2,128,16]{1,2,0:T(8,128)S(1)}, f32[2,128,16]{1,2,0:T(8,128)}, u32[]{:S(2)}) copy-start(f32[2,128,16]{1,2,0:T(8,128)} %convolution_subtract_fusion.21) | copy-start | bytes 49156
  313.6 94.6 %copy-start.22 = (f32[2,128,16]{1,2,0:T(8,128)S(1)}, f32[2,128,16]{1,2,0:T(8,128)}, u32[]{:S(2)}) copy-start(f32[2,128,16]{1,2,0:T(8,128)} %convolution_subtract_fusion.18) | copy-start | bytes 49156
  313.6 94.9 %copy-start.23 = (f32[2,128,16]{1,2,0:T(8,128)S(1)}, f32[2,128,16]{1,2,0:T(8,128)}, u32[]{:S(2)}) copy-start(f32[2,128,16]{1,2,0:T(8,128)} %convolution_subtract_fusion.20) | copy-start | bytes 49156
  359.5 52.5 %copy-start.6 = (f32[2,128,128]{2,1,0:T(8,128)S(1)}, f32[2,128,128]{2,1,0:T(8,128)}, u32[]{:S(2)}) copy-start(f32[2,128,128]{2,1,0:T(8,128)} %copy-done.5) | copy-start | bytes 393220
  411.2 22.9 %copy-start.30 = (pred[2]{0:T(512)(128)(4,1)S(1)}, pred[2]{0:T(512)(128)(4,1)}, u32[]{:S(2)}) copy-start(pred[2]{0:T(512)(128)(4,1)} %compare_and_fusion.2) | copy-start | bytes 10
  435.6 8.6 %copy-start.1 = (bf16[1024,16]{0,1:T(8,128)(2,1)S(1)}, bf16[1024,16]{0,1:T(8,128)(2,1)}, u32[]{:S(2)}) copy-start(bf16[1024,16]{0,1:T(8,128)(2,1)} %param.16) | copy-start | bytes 98308
  (6 other events, 6.1 us)
Sparse Core Ops, SparseCore 0:
  64.8 126.1 reduce-scatter.1

commit v3 on v2

--- a/solution.py
+++ b/solution.py
@@ -1,6 +1,8 @@
 import jax
 import jax.numpy as jnp
 from jax import lax
+from jax.experimental import pallas as pl
+from jax.experimental.pallas import tpu as pltpu
 from jax.sharding import PartitionSpec as P
 
 SNPS = 500
@@ -51,15 +53,57 @@
     return jnp.einsum(spec, left, right, precision=HIGH, preferred_element_type=jnp.float32)
 
 
+def inverse_factor_kernel(d_ref, w_ref, a_scr):
+    count, n, _ = d_ref.shape
+    a_scr[...] = d_ref[...]
+    sub = lax.broadcasted_iota(jnp.int32, (n, n), 0)
+    lane = lax.broadcasted_iota(jnp.int32, (n, n), 1)
+    eye = jnp.where(sub == lane, 1.0, 0.0).astype(jnp.float32)
+    for s in range(count):
+        w_ref[s] = eye
+    row_lane = lax.broadcasted_iota(jnp.int32, (1, n), 1)
+    col_sub = lax.broadcasted_iota(jnp.int32, (n, 1), 0)
+
+    def step(j, carry):
+        for s in range(count):
+            a = a_scr[s]
+            row = jnp.sum(jnp.where(sub == j, a, 0.0), axis=0, keepdims=True)
+            piv = jnp.sum(jnp.where(row_lane == j, row, 0.0), axis=1, keepdims=True)
+            scale = 1.0 / jnp.sqrt(piv)
+            col = jnp.sum(jnp.where(lane == j, a, 0.0), axis=1, keepdims=True)
+            lcol = jnp.where(col_sub >= j, col * scale, 0.0)
+            lrow = jnp.where(row_lane >= j, row * scale, 0.0)
+            a_scr[s] = a - lcol * lrow
+            r = w_ref[s]
+            xrow = jnp.sum(jnp.where(sub == j, r, 0.0), axis=0, keepdims=True) * scale
+            strict = jnp.where(col_sub > j, lcol, 0.0)
+            w_ref[s] = jnp.where(sub == j, xrow, r - strict * xrow)
+        return carry
+
+    lax.fori_loop(0, n, step, 0)
+
+
+def inverse_factor(block):
+    count, n, _ = block.shape
+    return pl.pallas_call(
+        inverse_factor_kernel,
+        out_shape=jax.ShapeDtypeStruct(block.shape, jnp.float32),
+        in_specs=[pl.BlockSpec(memory_space=pltpu.VMEM)],
+        out_specs=pl.BlockSpec(memory_space=pltpu.VMEM),
+        scratch_shapes=[pltpu.VMEM(block.shape, jnp.float32)],
+        cost_estimate=pl.CostEstimate(
+            flops=12 * count * n * n * n, bytes_accessed=8 * count * n * n, transcendentals=count * n
+        ),
+    )(block)
+
+
 def block_solve(tiles, target, panels):
     pairs = tile_pairs(panels)
     upper = {pair: tiles[:, index] for index, pair in enumerate(pairs)}
-    eye = jnp.broadcast_to(jnp.eye(PANEL, dtype=jnp.float32), (tiles.shape[0], PANEL, PANEL))
     lower = {}
     inverse = {}
     for p in range(panels):
-        factor = jnp.linalg.cholesky(upper[(p, p)])
-        inv = lax.linalg.triangular_solve(factor, eye, left_side=True, lower=True)
+        inv = inverse_factor(upper[(p, p)])
         inverse[p] = inv
         for q in range(p + 1, panels):
             lower[(q, p)] = mm("sji,skj->sik", upper[(p, q)], inv)

time: 456 us -> 355 us (0.78)
  other arithmetic: 206 us -> 19.8 us
  Pallas kernels: 0 us -> 87.9 us
  local copies, waits for them, and re-layouts: 28.5 us -> 23.8 us
    another operation x22 -> x0, other arithmetic: 182 us -> none  [the longest x13 97.8 us: block_solve(): factor = jnp.linalg.cholesky(upper[p, p])]
    pallas_call x0 -> x4, Pallas kernels: none -> 87.9 us  [inverse_factor(): pl.pallas_call(inverse_factor_kernel, out_shape=jax.ShapeDtypeStruct(bloc...]
    dot_general x36, matrix products: 26.5 us -> 33.4 us  [mm(): jnp.einsum(spec, left, right, precision=HIGH, preferred_element_type=jnp....]
where the time goes in v3:
time: 355 us; the launch traced here: 354 us
  waiting for transfers between devices  121 us (34%)
  Pallas kernels  87.9 us (25%)
  matrix products  58.2 us (16%)
  blocking collectives  28.2 us (8%)
  local copies, waits for them, and re-layouts  23.8 us (7%)
  other arithmetic  19.8 us (6%)
  between operations  14.9 us (4%)
    reduce_scatter x1, waiting for transfers between devices, shards(): lax.psum_scatter(payload, 'sample', scatter_dimension=0, tiled=True)[0]  121 us
    pallas_call x4, Pallas kernels, inverse_factor(): pl.pallas_call(inverse_factor_kernel, out_shape=jax.ShapeDtypeStruct(bloc...  87.9 us
    dot_general x36, matrix products, mm(): jnp.einsum(spec, left, right, precision=HIGH, preferred_element_type=jnp....  33.4 us
    all_gather x1, blocking collectives, shards(): collected = lax.all_gather(solved, 'sample', axis=0, tiled=True)  21.2 us
    dot_general x44, matrix products, inner_products(): lax.dot_general(left_cols, right_cols, (((0,), (0,)), ((), ())), preferre...  14.2 us
    concatenate x1, other arithmetic, shards(): payload = jnp.concatenate([gram_rows, cross_rows], axis=1)  9.16 us
    dot_general x1, matrix products, shards(): jnp.einsum('wjm,jmtab->wtab', coefficient, local_grams, precision=HIGH)  7.94 us
    reshape x1, local copies, waits for them, and re-layouts, shards(): gram_rows = gram_payload.reshape(devices, span * tile_count * PANEL, PANEL)  7.29 us
  transfers between devices with their start and end apart: 1, of which 1 were waited for; matrix products, arithmetic and copies ran while one was open for 1% of the time, Pallas kernels for 0%

profile of v3, /device:TPU:0, one launch (start us, length us, event | category | flops | bytes accessed | tf_op | source)
XLA Modules:
  0.0 353.6 jit_solution(6278416898834113782)
XLA Ops:
  8.6 2.7 divide_convert_fusion
  13.0 2.3 slice_select_fusion
  18.0 1.3 convolution_bitcast_fusion
  19.3 3.6 %copy.52 = f32[16,512,16]{2,1,0:T(8,128)} copy(f32[16,512,16]{1,0,2:T(8,128)} %convolution_bitcast_fusion) | data formatting | bytes 1048576 | tf_op jit(solution)/shard_map/wjm,jmic->wic/dot_general | solution.py:199
  22.9 3.9 %reshape.571 = f32[16,64,128]{2,1,0:T(8,128)} reshape(f32[16,512,16]{2,1,0:T(8,128)} %copy.52) | data formatting | bytes 1048576 | tf_op jit(solution)/shard_map/reshape | solution.py:201
  26.8 1.3 fusion.11
  39.8 7.9 %fusion = f32[16,10,128,128,1]{3,0,4,2,1:T(8,128)S(1)} fusion(f32[2,2,10,128,128]{4,3,2,0,1:T(8,128)S(1)} %pad_maximum_fusion.1, pred[16,1,2]{0,2,1:T(4,128)(4,1)S(1)} %get-tuple-element.43, pred[16,1,2]{0,2,1:T(4,128)(4,1)S(1)} %get-tuple-element.42), kind=kOutput, calls=%fused_computation.8 | convolution fusion | flops 125829184 | bytes 13107264 | tf_op jit(solution)/shard_map/wjm,jmtab->wtab/dot_general | solution.py:198
  47.8 7.3 %copy.53 = f32[16,1280,128]{2,1,0:T(8,128)} copy(f32[16,1280,128]{2,0,1:T(8,128)S(1)} %bitcast.338) | data formatting | bytes 20971520 | tf_op jit(solution)/shard_map/reshape | solution.py:200
  55.1 9.2 %pad_maximum_fusion = f32[16,1344,128]{2,1,0:T(8,128)} fusion(f32[16,64,128]{2,1,0:T(8,128)S(1)} %copy-done.13, f32[16,1280,128]{2,1,0:T(8,128)} %copy.53), kind=kLoop, calls=%fused_computation.5 | loop fusion | flops 2752512 | bytes 22020096 | tf_op jit(solution)/shard_map/concatenate | solution.py:202
  69.8 120.8 %reduce-scatter.2.cloned.1.call-done = f32[1,1344,128]{2,1,0:T(8,128)} async-done(((f32[16,1344,128]{2,1,0:T(8,128)}), f32[1,1344,128]{2,1,0:T(8,128)}) %reduce-scatter.2.cloned.1.call-update) | async-done | bytes 688144 | tf_op jit(solution)/shard_map/reduce_scatter | solution.py:203
  192.9 22.0 %shard_map.109 = f32[2,128,128]{2,1,0:T(8,128)} custom-call(f32[2,128,128]{2,1,0:T(8,128)} %slice_bitcast_fusion.12.d_ref), custom_call_target="tpu_custom_call" | custom-call | flops 50331648 | bytes 262144 | tf_op jit(solution)/shard_map/pallas_call | solution.py:88
  214.8 1.4 fusion.96
  216.2 1.4 fusion.98
  217.6 1.3 convolution_subtract_fusion.2
  218.9 1.3 convolution_subtract_fusion.4
  220.2 2.0 convolution_subtract_fusion.9.d_ref
  222.2 1.3 fusion.97
  223.5 1.3 convolution_subtract_fusion.5
  224.8 1.3 convolution_subtract_fusion.8
  226.1 2.0 convolution_subtract_fusion.7
  230.9 22.0 %shard_map.110 = f32[2,128,128]{2,1,0:T(8,128)} custom-call(f32[2,128,128]{2,1,0:T(8,128)} %convolution_subtract_fusion.9.d_ref), custom_call_target="tpu_custom_call" | custom-call | flops 50331648 | bytes 262144 | tf_op jit(solution)/shard_map/pallas_call | solution.py:88
  252.8 1.4 fusion.146
  254.2 1.3 fusion.144
  256.9 1.9 convolution_subtract_fusion.6.d_ref
  258.9 22.0 %shard_map.111 = f32[2,128,128]{2,1,0:T(8,128)} custom-call(f32[2,128,128]{2,1,0:T(8,128)} %convolution_subtract_fusion.6.d_ref), custom_call_target="tpu_custom_call" | custom-call | flops 50331648 | bytes 262144 | tf_op jit(solution)/shard_map/pallas_call | solution.py:88
  280.9 1.4 fusion.147
  282.2 2.0 convolution_subtract_fusion.d_ref
  284.2 22.0 %shard_map.112 = f32[2,128,128]{2,1,0:T(8,128)} custom-call(f32[2,128,128]{2,1,0:T(8,128)} %convolution_subtract_fusion.d_ref), custom_call_target="tpu_custom_call" | custom-call | flops 50331648 | bytes 262144 | tf_op jit(solution)/shard_map/pallas_call | solution.py:88
  308.6 1.2 fusion.145
  310.1 1.2 fusion.148
  314.6 21.2 %all_gather.3 = bf16[32,500,16]{1,2,0:T(8,128)(2,1)S(1)} all-gather(bf16[2,500,16]{1,2,0:T(8,128)(2,1)S(1)} %pad_maximum_fusion.4), channel_id=1, replica_groups=mesh['sample'=16,'block'=2] {'sample'}, dimensions={0}, use_global_device_ids=true | all-gather | bytes 544000 | tf_op jit(solution)/shard_map/all_gather | solution.py:231
  339.0 7.0 %all_to_all.18 = bf16[16,4,1024]{2,1,0:T(4,128)(2,1)S(1)} all-to-all(bf16[16,4,1024]{2,1,0:T(4,128)(2,1)S(1)} %pad_maximum_fusion.3), channel_id=1, replica_groups=mesh['sample'=16,'block'=2] {'block'}, dimensions={0} | all-to-all | bytes 262144 | tf_op jit(solution)/shard_map/all_to_all | solution.py:244
  (184 shorter events, 38.8 us)
Async XLA Ops:
  6.5 5.0 %copy-start = (bf16[1024,16]{0,1:T(8,128)(2,1)S(1)}, bf16[1024,16]{0,1:T(8,128)(2,1)}, u32[]{:S(2)}) copy-start(bf16[1024,16]{0,1:T(8,128)(2,1)} %param.13) | copy-start | bytes 98308
  6.5 184.0 %reduce-scatter.2.cloned.1.call-start = ((), (), s32[]{:S(2)}) async-start(), calls=%async_computation.2 | async-start | bytes 11698176 | tf_op jit(solution)/shard_map/reduce_scatter | solution.py:203
  12.2 0.8 copy-start.22
  12.2 3.1 copy-start.19
  15.3 2.7 copy-start.6
  15.3 2.7 copy-start.8
  15.3 2.7 copy-start.15
  15.3 2.6 copy-start.25
  15.3 2.7 copy-start.24
  26.8 2.5 copy-start.11
  30.5 1.2 copy-start.10
  33.4 1.2 copy-start.9
  33.4 1.5 copy-start.16
  33.5 1.7 copy-start.18
  35.9 1.4 copy-start.7
  35.9 1.4 copy-start.17
  47.8 7.3 %copy-start.13 = (f32[16,64,128]{2,1,0:T(8,128)S(1)}, f32[16,64,128]{2,1,0:T(8,128)}, u32[]{:S(2)}) copy-start(f32[16,64,128]{2,1,0:T(8,128)} %reshape.571) | copy-start | bytes 1572868
  64.2 0.7 copy-start.26
  64.3 1.3 copy-start.1
  64.3 1.9 copy-start.2
  64.3 5.3 %copy-start.23 = (f32[10]{0:T(128)S(1)}, f32[10]{0:T(128)}, u32[]{:S(2)}) copy-start(f32[10]{0:T(128)} %constant.231) | copy-start | bytes 124
  192.1 22.7 %copy-start.3 = (f32[2,10,128,128]{3,2,0,1:T(8,128)}, f32[2,10,128,128]{3,2,0,1:T(8,128)S(1)}, u32[]{:S(2)}) copy-start(f32[2,10,128,128]{3,2,0,1:T(8,128)S(1)} %multiply_add_fusion) | copy-start | bytes 3932164
  214.8 7.3 %copy-start.4 = (f32[2,128,128]{2,1,0:T(8,128)S(1)}, f32[2,128,128]{2,1,0:T(8,128)}, u32[]{:S(2)}) copy-start(f32[2,128,128]{2,1,0:T(8,128)} %shard_map.109) | copy-start | bytes 393220
  216.2 11.8 %slice-start = ((f32[1,1344,128]{2,1,0:T(8,128)}), f32[1,64,128]{2,1,0:T(8,128)S(1)}, s32[]{:S(2)}) async-start(f32[1,1344,128]{2,1,0:T(8,128)} %reduce-scatter.2.cloned.1.call-done), calls=%async_computation.3 | async-start | bytes 65536 | tf_op jit(solution)/shard_map/slice | solution.py:206
  217.6 10.8 %copy-start.5 = (f32[2,128,128]{2,1,0:T(8,128)S(1)}, f32[2,128,128]{2,1,0:T(8,128)}, u32[]{:S(2)}) copy-start(f32[2,128,128]{2,1,0:T(8,128)} %shard_map.109) | copy-start | bytes 393220
  252.8 53.3 %copy-start.12 = (f32[2,128,128]{2,1,0:T(8,128)S(1)}, f32[2,128,128]{2,1,0:T(8,128)}, u32[]{:S(2)}) copy-start(f32[2,128,128]{2,1,0:T(8,128)} %shard_map.110) | copy-start | bytes 393220
  280.9 31.9 %copy-start.14 = (f32[2,128,128]{2,1,0:T(8,128)S(1)}, f32[2,128,128]{2,1,0:T(8,128)}, u32[]{:S(2)}) copy-start(f32[2,128,128]{2,1,0:T(8,128)} %shard_map.111) | copy-start | bytes 393220
  313.7 22.9 %copy-start.21 = (pred[2]{0:T(512)(128)(4,1)S(1)}, pred[2]{0:T(512)(128)(4,1)}, u32[]{:S(2)}) copy-start(pred[2]{0:T(512)(128)(4,1)} %compare_and_fusion.2) | copy-start | bytes 10
  338.0 0.7 copy-start.20
Sparse Core Ops, SparseCore 0:
  64.4 126.1 reduce-scatter.1

commit v4 on v3

--- a/solution.py
+++ b/solution.py
@@ -166,20 +166,19 @@
     slot_masks = [fold_of == slot_folds[0], fold_of == slot_folds[1]]
     picked = jnp.minimum(jnp.stack(slot_folds), FOLDS - 1)
 
-    gram_parts = []
-    cross_parts = []
-    for member in range(member_count):
-        columns = jnp.pad(column_sets[member], ((0, 0), (0, padded_width - SNPS)))
-        slot_grams = []
-        slot_crosses = []
-        for slot in range(2):
+    slot_rows = []
+    for slot in range(2):
+        member_rows = []
+        for member in range(member_count):
+            columns = jnp.pad(column_sets[member], ((0, 0), (0, padded_width - SNPS)))
             masked = jnp.where(slot_masks[slot][:, None], columns, jnp.zeros_like(columns))
-            slot_grams.append(tile_grams(masked, columns, panels))
-            slot_crosses.append(inner_products(masked, ordered))
-        gram_parts.append(jnp.stack(slot_grams))
-        cross_parts.append(jnp.stack(slot_crosses))
-    local_grams = jnp.stack(gram_parts, axis=1)
-    local_crosses = jnp.stack(cross_parts, axis=1)
+            tiles = tile_grams(masked, columns, panels)
+            cross = jnp.stack(
+                [inner_products(ordered, masked[:, p * PANEL : (p + 1) * PANEL]) for p in range(panels)]
+            )
+            member_rows.append(jnp.concatenate([tiles.reshape(-1, PANEL), cross.reshape(-1, PANEL)]))
+        slot_rows.append(jnp.stack(member_rows))
+    local_rows = jnp.stack(slot_rows)
 
     wanted = []
     for device in range(devices):
@@ -195,15 +194,14 @@
         ],
         axis=1,
     ).astype(jnp.float32)
-    gram_payload = jnp.einsum("wjm,jmtab->wtab", coefficient, local_grams, precision=HIGH)
-    cross_payload = jnp.einsum("wjm,jmic->wic", coefficient, local_crosses, precision=HIGH)
-    gram_rows = gram_payload.reshape(devices, span * tile_count * PANEL, PANEL)
-    cross_rows = cross_payload.reshape(devices, span * padded_width * traits // PANEL, PANEL)
-    payload = jnp.concatenate([gram_rows, cross_rows], axis=1)
+    payload = jnp.sum(coefficient[:, :, :, None, None] * local_rows[None], axis=(1, 2))
+    row_count = local_rows.shape[2]
+    payload = payload.reshape(devices, span * row_count, PANEL)
     reduced = lax.psum_scatter(payload, "sample", scatter_dimension=0, tiled=True)[0]
-    split = span * tile_count * PANEL
-    mine_grams = reduced[:split].reshape(span, tile_count, PANEL, PANEL)
-    mine_crosses = reduced[split:].reshape(span, padded_width, traits)
+    reduced = reduced.reshape(span, row_count, PANEL)
+    split = tile_count * PANEL
+    mine_grams = reduced[:, :split].reshape(span, tile_count, PANEL, PANEL)
+    mine_crosses = reduced[:, split:].reshape(span, panels, traits, PANEL)
 
     owned_ids = jnp.minimum(me * share + lax.broadcasted_iota(jnp.int32, (share,), 0), systems - 1)
     pair_ids = owned_ids // ridge_count
@@ -226,7 +224,8 @@
         + (1.0 - ridge[:, None, None]) * pad_diag[None, :, :]
     )
     system = rest_tiles / chosen_counts[:, None, None, None] + diag_add[:, :, :, None] * identity
-    target = rest_crosses / chosen_counts[:, None, None]
+    target = jnp.swapaxes(rest_crosses, 2, 3).reshape(share, padded_width, traits)
+    target = target / chosen_counts[:, None, None]
     solved = block_solve(system, target, panels)[:, :SNPS].astype(jnp.bfloat16)
     collected = lax.all_gather(solved, "sample", axis=0, tiled=True)
     every_weights = collected[:systems].reshape(FOLDS, member_count, ridge_count, SNPS, traits)

time: 355 us -> 338 us (0.952)
  matrix products: 58.2 us -> 43.4 us
  local copies, waits for them, and re-layouts: 23.8 us -> 9.07 us
  other arithmetic: 19.8 us -> 33.3 us
    reduce_sum x0 -> x1, other arithmetic: none -> 20.1 us  [shards(): jnp.sum(coefficient[:, :, :, None, None] * local_rows[None], axis=(1, 2))]
    reshape x2 -> x1, local copies, waits for them, and re-layouts: 11.2 us -> 0.03 us  [shards(): jnp.swapaxes(rest_crosses, 2, 3).reshape(share, padded_width, traits)]
    dot_general x2 -> x0, matrix products: 9.23 us -> none  [the longest x1 7.94 us: shards(): jnp.einsum('wjm,jmtab->wtab', coefficient, local_grams, precision=HIGH)]
    concatenate x1 -> x0, other arithmetic: 9.16 us -> none  [shards(): payload = jnp.concatenate([gram_rows, cross_rows], axis=1)]
    dot_general x36, matrix products: 33.4 us -> 29.2 us  [mm(): jnp.einsum(spec, left, right, precision=HIGH, preferred_element_type=jnp....]
    dot_general x1 -> x0, local copies, waits for them, and re-layouts: 3.55 us -> none  [shards(): jnp.einsum('wjm,jmic->wic', coefficient, local_crosses, precision=HIGH)]
    dot_general x44 -> x56, matrix products: 14.2 us -> 12.8 us  [inner_products(): lax.dot_general(left_cols, right_cols, (((0,), (0,)), ((), ())), preferre...]
where the time goes in v4:
time: 338 us
  waiting for transfers between devices  121 us (36%)
  Pallas kernels  88 us (26%)
  matrix products  43.4 us (13%)
  other arithmetic  33.3 us (10%)
  blocking collectives  28.2 us (8%)
  between operations  14.9 us (4%)
  local copies, waits for them, and re-layouts  9.07 us (3%)
    reduce_scatter x1, waiting for transfers between devices, shards(): lax.psum_scatter(payload, 'sample', scatter_dimension=0, tiled=True)[0]  121 us
    pallas_call x4, Pallas kernels, inverse_factor(): pl.pallas_call(inverse_factor_kernel, out_shape=jax.ShapeDtypeStruct(bloc...  88 us
    dot_general x36, matrix products, mm(): jnp.einsum(spec, left, right, precision=HIGH, preferred_element_type=jnp....  29.2 us
    all_gather x1, blocking collectives, shards(): collected = lax.all_gather(solved, 'sample', axis=0, tiled=True)  21.2 us
    reduce_sum x1, other arithmetic, shards(): jnp.sum(coefficient[:, :, :, None, None] * local_rows[None], axis=(1, 2))  20.1 us
    dot_general x56, matrix products, inner_products(): lax.dot_general(left_cols, right_cols, (((0,), (0,)), ((), ())), preferre...  12.8 us
    all_to_all x1, blocking collectives, shards(): lax.all_to_all(local_preds, 'block', split_axis=0, concat_axis=1, tiled=T...  7.01 us
  transfers between devices with their start and end apart: 1, of which 1 were waited for; matrix products, arithmetic and copies ran while one was open for 1% of the time, Pallas kernels for 0%

profile of v4, /device:TPU:0, one launch (start us, length us, event | category | flops | bytes accessed | tf_op | source)
XLA Modules:
  0.0 337.6 jit_solution(10082121013001017138)
XLA Ops:
  8.6 2.7 divide_convert_fusion
  12.2 1.0 broadcast_select_fusion.2
  27.4 1.1 maximum_bitcast_fusion.2
  28.6 1.2 maximum_bitcast_fusion.3
  31.2 20.1 %multiply_reduce_fusion = f32[16,1344,128]{2,1,0:T(8,128)} fusion(f32[2,2,1344,128]{3,2,1,0:T(8,128)S(1)} %pad_maximum_fusion, f32[16,2,2]{2,1,0:T(2,128)S(1)} %copy.53), kind=kLoop, calls=%fused_computation.5 | loop fusion | flops 19267584 | bytes 13762816 | tf_op jit(solution)/shard_map/reduce_sum | solution.py:197
  57.0 120.6 %reduce-scatter.2.cloned.1.call-done = f32[1,1344,128]{2,1,0:T(8,128)} async-done(((f32[16,1344,128]{2,1,0:T(8,128)}), f32[1,1344,128]{2,1,0:T(8,128)}) %reduce-scatter.2.cloned.1.call-update) | async-done | bytes 688144 | tf_op jit(solution)/shard_map/reduce_scatter | solution.py:200
  177.6 1.1 slice.323
  179.9 22.0 %shard_map.109 = f32[2,128,128]{2,1,0:T(8,128)} custom-call(f32[2,128,128]{2,1,0:T(8,128)} %slice_bitcast_fusion.12.d_ref), custom_call_target="tpu_custom_call" | custom-call | flops 50331648 | bytes 262144 | tf_op jit(solution)/shard_map/pallas_call | solution.py:88
  201.9 1.3 fusion.111
  203.2 1.4 fusion.112
  206.1 1.2 fusion.134
  207.3 2.0 convolution_subtract_fusion.9.d_ref
  209.9 1.3 convolution_subtract_fusion.8
  211.2 1.3 convolution_subtract_fusion.7
  212.5 1.3 fusion.110
  214.1 1.3 convolution_subtract_fusion.4
  215.4 1.3 convolution_subtract_fusion.5
  216.7 1.3 convolution_subtract_fusion.2
  218.0 22.0 %shard_map.110 = f32[2,128,128]{2,1,0:T(8,128)} custom-call(f32[2,128,128]{2,1,0:T(8,128)} %convolution_subtract_fusion.9.d_ref), custom_call_target="tpu_custom_call" | custom-call | flops 50331648 | bytes 262144 | tf_op jit(solution)/shard_map/pallas_call | solution.py:88
  240.0 1.2 fusion.154
  241.2 1.3 fusion.155
  242.5 1.0 convolution_subtract_fusion.6.d_ref
  243.6 22.0 %shard_map.111 = f32[2,128,128]{2,1,0:T(8,128)} custom-call(f32[2,128,128]{2,1,0:T(8,128)} %convolution_subtract_fusion.6.d_ref), custom_call_target="tpu_custom_call" | custom-call | flops 50331648 | bytes 262144 | tf_op jit(solution)/shard_map/pallas_call | solution.py:88
  265.6 1.3 fusion.157
  267.9 1.2 fusion.156
  269.2 1.3 fusion.158
  270.9 1.0 convolution_subtract_fusion.d_ref
  271.9 22.0 %shard_map.112 = f32[2,128,128]{2,1,0:T(8,128)} custom-call(f32[2,128,128]{2,1,0:T(8,128)} %convolution_subtract_fusion.d_ref), custom_call_target="tpu_custom_call" | custom-call | flops 50331648 | bytes 262144 | tf_op jit(solution)/shard_map/pallas_call | solution.py:88
  294.2 1.2 fusion.159
  295.4 1.1 fusion.151
  298.7 21.2 %all_gather.3 = bf16[32,500,16]{1,2,0:T(8,128)(2,1)S(1)} all-gather(bf16[2,500,16]{1,2,0:T(8,128)(2,1)S(1)} %pad_maximum_fusion.2), channel_id=1, replica_groups=mesh['sample'=16,'block'=2] {'sample'}, dimensions={0}, use_global_device_ids=true | all-gather | bytes 544000 | tf_op jit(solution)/shard_map/all_gather | solution.py:230
  323.0 7.0 %all_to_all.18 = bf16[16,4,1024]{2,1,0:T(4,128)(2,1)S(1)} all-to-all(bf16[16,4,1024]{2,1,0:T(4,128)(2,1)S(1)} %pad_maximum_fusion.1), channel_id=1, replica_groups=mesh['sample'=16,'block'=2] {'block'}, dimensions={0} | all-to-all | bytes 262144 | tf_op jit(solution)/shard_map/all_to_all | solution.py:243
  (191 shorter events, 34.2 us)
Async XLA Ops:
  6.5 5.1 %copy-start = (bf16[1024,16]{0,1:T(8,128)(2,1)S(1)}, bf16[1024,16]{0,1:T(8,128)(2,1)}, u32[]{:S(2)}) copy-start(bf16[1024,16]{0,1:T(8,128)(2,1)} %param.13) | copy-start | bytes 98308
  6.5 171.1 %reduce-scatter.2.cloned.1.call-start = ((), (), s32[]{:S(2)}) async-start(), calls=%async_computation.2 | async-start | bytes 11698176 | tf_op jit(solution)/shard_map/reduce_scatter | solution.py:200
  11.3 0.9 copy-start.18
  11.6 1.6 copy-start.13
  19.9 1.0 copy-start.12
  22.1 1.4 copy-start.11
  24.2 1.0 copy-start.9
  25.7 1.6 copy-start.21
  25.7 1.6 copy-start.20
  26.4 0.8 copy-start.7
  28.6 1.3 copy-start.10
  29.8 1.1 copy-start.8
  51.3 0.7 copy-start.22
  51.3 1.3 copy-start.1
  51.3 1.9 copy-start.2
  51.3 5.5 %copy-start.19 = (f32[10]{0:T(128)S(1)}, f32[10]{0:T(128)}, u32[]{:S(2)}) copy-start(f32[10]{0:T(128)} %constant.232) | copy-start | bytes 124
  55.4 124.5 %copy-start.15 = (pred[2]{0:T(512)(128)(4,1)}, pred[2]{0:T(512)(128)(4,1)S(1)}, u32[]{:S(2)}) copy-start(pred[2]{0:T(512)(128)(4,1)S(1)} %compare_and_fusion.1) | copy-start | bytes 10
  56.8 123.1 %copy-start.16 = (f32[2]{0:T(128)}, f32[2]{0:T(128)S(1)}, u32[]{:S(2)}) copy-start(f32[2]{0:T(128)S(1)} %and_select_fusion.4) | copy-start | bytes 28
  177.6 27.0 %slice-start = ((f32[1,1344,128]{2,1,0:T(8,128)}), f32[1,64,128]{2,1,0:T(8,128)S(1)}, s32[]{:S(2)}) async-start(f32[1,1344,128]{2,1,0:T(8,128)} %reduce-scatter.2.cloned.1.call-done), calls=%async_computation.3 | async-start | bytes 65536 | tf_op jit(solution)/shard_map/slice | solution.py:204
  179.2 22.7 %copy-start.3 = (f32[2,10,128,128]{3,2,0,1:T(8,128)}, f32[2,10,128,128]{3,2,0,1:T(8,128)S(1)}, u32[]{:S(2)}) copy-start(f32[2,10,128,128]{3,2,0,1:T(8,128)S(1)} %multiply_add_fusion) | copy-start | bytes 3932164
  203.2 9.3 %copy-start.4 = (f32[2,128,128]{2,1,0:T(8,128)S(1)}, f32[2,128,128]{2,1,0:T(8,128)}, u32[]{:S(2)}) copy-start(f32[2,128,128]{2,1,0:T(8,128)} %shard_map.109) | copy-start | bytes 393220
  265.6 31.3 %copy-start.6 = (f32[2,128,128]{2,1,0:T(8,128)S(1)}, f32[2,128,128]{2,1,0:T(8,128)}, u32[]{:S(2)}) copy-start(f32[2,128,128]{2,1,0:T(8,128)} %shard_map.111) | copy-start | bytes 393220
  266.9 30.6 %copy-start.5 = (f32[2,128,128]{2,1,0:T(8,128)S(1)}, f32[2,128,128]{2,1,0:T(8,128)}, u32[]{:S(2)}) copy-start(f32[2,128,128]{2,1,0:T(8,128)} %shard_map.110) | copy-start | bytes 393220
  297.8 22.9 %copy-start.17 = (pred[2]{0:T(512)(128)(4,1)S(1)}, pred[2]{0:T(512)(128)(4,1)}, u32[]{:S(2)}) copy-start(pred[2]{0:T(512)(128)(4,1)} %compare_and_fusion.2) | copy-start | bytes 10
  321.8 0.9 copy-start.14
Sparse Core Ops, SparseCore 0:
  51.4 126.1 reduce-scatter.1

commit v5 on v4

--- a/solution.py
+++ b/solution.py
@@ -194,7 +194,11 @@
         ],
         axis=1,
     ).astype(jnp.float32)
-    payload = jnp.sum(coefficient[:, :, :, None, None] * local_rows[None], axis=(1, 2))
+    payload = None
+    for slot in range(2):
+        for member in range(member_count):
+            term = coefficient[:, slot, member][:, None, None] * local_rows[slot, member][None]
+            payload = term if payload is None else payload + term
     row_count = local_rows.shape[2]
     payload = payload.reshape(devices, span * row_count, PANEL)
     reduced = lax.psum_scatter(payload, "sample", scatter_dimension=0, tiled=True)[0]

time: 338 us -> 321 us (0.950)
  other arithmetic: 33.3 us -> 15.6 us
    reduce_sum x1 -> x0, other arithmetic: 20.1 us -> none  [shards(): jnp.sum(coefficient[:, :, :, None, None] * local_rows[None], axis=(1, 2))]
    add x0 -> x1, other arithmetic: none -> 7.18 us  [shards(): payload = term if payload is None else payload + term]
where the time goes in v5:
time: 321 us
  waiting for transfers between devices  122 us (38%)
  Pallas kernels  87.9 us (27%)
  matrix products  43.5 us (14%)
  blocking collectives  28.2 us (9%)
  other arithmetic  15.6 us (5%)
  between operations  14.9 us (5%)
  local copies, waits for them, and re-layouts  8.81 us (3%)
    reduce_scatter x1, waiting for transfers between devices, shards(): lax.psum_scatter(payload, 'sample', scatter_dimension=0, tiled=True)[0]  122 us
    pallas_call x4, Pallas kernels, inverse_factor(): pl.pallas_call(inverse_factor_kernel, out_shape=jax.ShapeDtypeStruct(bloc...  87.9 us
    dot_general x36, matrix products, mm(): jnp.einsum(spec, left, right, precision=HIGH, preferred_element_type=jnp....  29.3 us
    all_gather x1, blocking collectives, shards(): collected = lax.all_gather(solved, 'sample', axis=0, tiled=True)  21.2 us
    dot_general x56, matrix products, inner_products(): lax.dot_general(left_cols, right_cols, (((0,), (0,)), ((), ())), preferre...  12.8 us
    add x1, other arithmetic, shards(): payload = term if payload is None else payload + term  7.18 us
    all_to_all x1, blocking collectives, shards(): lax.all_to_all(local_preds, 'block', split_axis=0, concat_axis=1, tiled=T...  7.01 us
  transfers between devices with their start and end apart: 1, of which 1 were waited for; matrix products, arithmetic and copies ran while one was open for 1% of the time, Pallas kernels for 0%

profile of v5, /device:TPU:0, one launch (start us, length us, event | category | flops | bytes accessed | tf_op | source)
XLA Modules:
  0.0 320.7 jit_solution(2152389019667294600)
XLA Ops:
  8.6 2.7 divide_convert_fusion
  12.2 1.0 broadcast_select_fusion.2
  27.6 7.2 %multiply_add_fusion = f32[16,1344,128]{2,1,0:T(8,128)} fusion(f32[1344,128]{1,0:T(8,128)S(1)} %get-tuple-element.33, f32[16]{0:T(128)S(1)} %get-tuple-element.46, f32[1344,128]{1,0:T(8,128)S(1)} %get-tuple-element.32, f32[16]{0:T(128)S(1)} %get-tuple-element.47, f32[1344,128]{1,0:T(8,128)S(1)} %get-tuple-element.31, f32[16]{0:T(128)S(1)} %get-tuple-element.48, ...), kind=kLoop, calls=%fused_computation.5 | loop fusion | flops 19267584 | bytes 13762816 | tf_op jit(solution)/shard_map/add | solution.py:201
  38.0 0.9 scatter_custom_fusion
  39.4 121.7 %reduce-scatter.2.cloned.1.call-done = f32[1,1344,128]{2,1,0:T(8,128)} async-done(((f32[16,1344,128]{2,1,0:T(8,128)}), f32[1,1344,128]{2,1,0:T(8,128)}) %reduce-scatter.2.cloned.1.call-update) | async-done | bytes 688144 | tf_op jit(solution)/shard_map/reduce_scatter | solution.py:204
  161.1 1.1 slice.363
  162.7 1.1 copy-done.3
  164.4 22.0 %shard_map.109 = f32[2,128,128]{2,1,0:T(8,128)} custom-call(f32[2,128,128]{2,1,0:T(8,128)} %slice_bitcast_fusion.16.d_ref), custom_call_target="tpu_custom_call" | custom-call | flops 50331648 | bytes 262144 | tf_op jit(solution)/shard_map/pallas_call | solution.py:88
  186.4 1.4 fusion.111
  187.8 1.4 fusion.112
  189.4 1.2 fusion.134
  190.6 2.0 convolution_subtract_fusion.9.d_ref
  193.2 1.3 convolution_subtract_fusion.8
  194.5 1.3 convolution_subtract_fusion.7
  195.8 1.3 fusion.110
  197.4 1.3 convolution_subtract_fusion.4
  198.7 1.3 convolution_subtract_fusion.5
  200.0 1.3 convolution_subtract_fusion.2
  201.3 22.0 %shard_map.110 = f32[2,128,128]{2,1,0:T(8,128)} custom-call(f32[2,128,128]{2,1,0:T(8,128)} %convolution_subtract_fusion.9.d_ref), custom_call_target="tpu_custom_call" | custom-call | flops 50331648 | bytes 262144 | tf_op jit(solution)/shard_map/pallas_call | solution.py:88
  223.3 1.2 fusion.154
  224.5 1.3 fusion.155
  225.8 1.0 convolution_subtract_fusion.6.d_ref
  226.9 22.0 %shard_map.111 = f32[2,128,128]{2,1,0:T(8,128)} custom-call(f32[2,128,128]{2,1,0:T(8,128)} %convolution_subtract_fusion.6.d_ref), custom_call_target="tpu_custom_call" | custom-call | flops 50331648 | bytes 262144 | tf_op jit(solution)/shard_map/pallas_call | solution.py:88
  248.8 1.3 fusion.157
  251.2 1.2 fusion.156
  252.4 1.3 fusion.158
  254.2 1.0 convolution_subtract_fusion.d_ref
  255.2 22.0 %shard_map.112 = f32[2,128,128]{2,1,0:T(8,128)} custom-call(f32[2,128,128]{2,1,0:T(8,128)} %convolution_subtract_fusion.d_ref), custom_call_target="tpu_custom_call" | custom-call | flops 50331648 | bytes 262144 | tf_op jit(solution)/shard_map/pallas_call | solution.py:88
  277.5 1.2 fusion.159
  278.7 1.1 fusion.151
  282.0 21.2 %all_gather.3 = bf16[32,500,16]{1,2,0:T(8,128)(2,1)S(1)} all-gather(bf16[2,500,16]{1,2,0:T(8,128)(2,1)S(1)} %pad_maximum_fusion.1), channel_id=1, replica_groups=mesh['sample'=16,'block'=2] {'sample'}, dimensions={0}, use_global_device_ids=true | all-gather | bytes 544000 | tf_op jit(solution)/shard_map/all_gather | solution.py:234
  306.1 7.0 %all_to_all.18 = bf16[16,4,1024]{2,1,0:T(4,128)(2,1)S(1)} all-to-all(bf16[16,4,1024]{2,1,0:T(4,128)(2,1)S(1)} %pad_maximum_fusion), channel_id=1, replica_groups=mesh['sample'=16,'block'=2] {'block'}, dimensions={0} | all-to-all | bytes 262144 | tf_op jit(solution)/shard_map/all_to_all | solution.py:247
  (170 shorter events, 29.5 us)
Async XLA Ops:
  6.5 5.1 %copy-start = (bf16[1024,16]{0,1:T(8,128)(2,1)S(1)}, bf16[1024,16]{0,1:T(8,128)(2,1)}, u32[]{:S(2)}) copy-start(bf16[1024,16]{0,1:T(8,128)(2,1)} %param.13) | copy-start | bytes 98308
  6.5 154.6 %reduce-scatter.2.cloned.1.call-start = ((), (), s32[]{:S(2)}) async-start(), calls=%async_computation.2 | async-start | bytes 11698176 | tf_op jit(solution)/shard_map/reduce_scatter | solution.py:204
  11.3 0.9 copy-start.7
  26.9 0.7 copy-start.10
  26.9 0.7 copy-start.9
  34.8 0.7 copy-start.11
  34.8 1.3 copy-start.1
  34.8 1.9 copy-start.2
  34.8 4.4 %copy-start.8 = (f32[10]{0:T(128)S(1)}, f32[10]{0:T(128)}, u32[]{:S(2)}) copy-start(f32[10]{0:T(128)} %constant.231) | copy-start | bytes 124
  161.1 28.0 %slice-start = ((f32[1,1344,128]{2,1,0:T(8,128)}), f32[1,64,128]{2,1,0:T(8,128)S(1)}, s32[]{:S(2)}) async-start(f32[1,1344,128]{2,1,0:T(8,128)} %reduce-scatter.2.cloned.1.call-done), calls=%async_computation.3 | async-start | bytes 65536 | tf_op jit(solution)/shard_map/slice | solution.py:208
  162.7 1.1 copy-start.3
  186.4 9.4 %copy-start.4 = (f32[2,128,128]{2,1,0:T(8,128)S(1)}, f32[2,128,128]{2,1,0:T(8,128)}, u32[]{:S(2)}) copy-start(f32[2,128,128]{2,1,0:T(8,128)} %shard_map.109) | copy-start | bytes 393220
  248.8 31.3 %copy-start.6 = (f32[2,128,128]{2,1,0:T(8,128)S(1)}, f32[2,128,128]{2,1,0:T(8,128)}, u32[]{:S(2)}) copy-start(f32[2,128,128]{2,1,0:T(8,128)} %shard_map.111) | copy-start | bytes 393220
  250.2 30.6 %copy-start.5 = (f32[2,128,128]{2,1,0:T(8,128)S(1)}, f32[2,128,128]{2,1,0:T(8,128)}, u32[]{:S(2)}) copy-start(f32[2,128,128]{2,1,0:T(8,128)} %shard_map.110) | copy-start | bytes 393220
Sparse Core Ops, SparseCore 0:
  34.9 126.1 reduce-scatter.1

commit v6 on v5

--- a/solution.py
+++ b/solution.py
@@ -99,30 +99,37 @@
 
 def block_solve(tiles, target, panels):
     pairs = tile_pairs(panels)
-    upper = {pair: tiles[:, index] for index, pair in enumerate(pairs)}
-    lower = {}
-    inverse = {}
+    bands = []
+    for row_tile in range(panels):
+        band = []
+        for col_tile in range(panels):
+            if row_tile <= col_tile:
+                band.append(tiles[:, pairs.index((row_tile, col_tile))])
+            else:
+                band.append(jnp.swapaxes(tiles[:, pairs.index((col_tile, row_tile))], 1, 2))
+        bands.append(jnp.concatenate(band, axis=2))
+    trailing = jnp.concatenate(bands, axis=1)
+    inverses = []
+    strips = []
     for p in range(panels):
-        inv = inverse_factor(upper[(p, p)])
-        inverse[p] = inv
-        for q in range(p + 1, panels):
-            lower[(q, p)] = mm("sji,skj->sik", upper[(p, q)], inv)
-        for r in range(p + 1, panels):
-            for q in range(r, panels):
-                upper[(r, q)] = upper[(r, q)] - mm("sik,sjk->sij", lower[(r, p)], lower[(q, p)])
+        inv = inverse_factor(trailing[:, :PANEL, :PANEL])
+        inverses.append(inv)
+        if p + 1 < panels:
+            strip = mm("sij,skj->sik", trailing[:, PANEL:, :PANEL], inv)
+            strips.append(strip)
+            trailing = trailing[:, PANEL:, PANEL:] - mm("sik,sjk->sij", strip, strip)
+    residual = target
     forward = []
     for p in range(panels):
-        rhs = target[:, p * PANEL : (p + 1) * PANEL]
-        for q in range(p):
-            rhs = rhs - mm("sij,sjc->sic", lower[(p, q)], forward[q])
-        forward.append(mm("sij,sjc->sic", inverse[p], rhs))
-    backward = [None] * panels
-    for p in reversed(range(panels)):
-        rhs = forward[p]
-        for q in range(p + 1, panels):
-            rhs = rhs - mm("sji,sjc->sic", lower[(q, p)], backward[q])
-        backward[p] = mm("sji,sjc->sic", inverse[p], rhs)
-    return jnp.concatenate(backward, axis=1)
+        y = mm("sij,sjc->sic", inverses[p], residual[:, :PANEL])
+        forward.append(y)
+        if p + 1 < panels:
+            residual = residual[:, PANEL:] - mm("sij,sjc->sic", strips[p], y)
+    solved = mm("sji,sjc->sic", inverses[panels - 1], forward[panels - 1])
+    for p in reversed(range(panels - 1)):
+        rhs = forward[p] - mm("sji,sjc->sic", strips[p], solved)
+        solved = jnp.concatenate([mm("sji,sjc->sic", inverses[p], rhs), solved], axis=1)
+    return solved
 
 
 def owned_layout(systems, devices, ridge_count):

time: 321 us -> 318 us (level)
  matrix products: 43.5 us -> 32.5 us
  local copies, waits for them, and re-layouts: 8.81 us -> 15.6 us
    dot_general x36 -> x20, matrix products: 29.3 us -> 18.3 us  [mm(): jnp.einsum(spec, left, right, precision=HIGH, preferred_element_type=jnp....]
    transpose x0 -> x2, local copies, waits for them, and re-layouts: none -> 3.32 us  [block_solve(): band.append(jnp.swapaxes(tiles[:, pairs.index((col_tile, row_tile))], 1, 2))]
where the time goes in v6:
time: 318 us; the launch traced here: 317 us
  waiting for transfers between devices  122 us (38%)
  Pallas kernels  88 us (28%)
  matrix products  32.5 us (10%)
  blocking collectives  28.2 us (9%)
  other arithmetic  16.3 us (5%)
  local copies, waits for them, and re-layouts  15.6 us (5%)
  between operations  14.9 us (5%)
    reduce_scatter x1, waiting for transfers between devices, shards(): lax.psum_scatter(payload, 'sample', scatter_dimension=0, tiled=True)[0]  122 us
    pallas_call x4, Pallas kernels, inverse_factor(): pl.pallas_call(inverse_factor_kernel, out_shape=jax.ShapeDtypeStruct(bloc...  88 us
    all_gather x1, blocking collectives, shards(): collected = lax.all_gather(solved, 'sample', axis=0, tiled=True)  21.2 us
    dot_general x20, matrix products, mm(): jnp.einsum(spec, left, right, precision=HIGH, preferred_element_type=jnp....  18.3 us
    dot_general x56, matrix products, inner_products(): lax.dot_general(left_cols, right_cols, (((0,), (0,)), ((), ())), preferre...  12.8 us
    add x1, other arithmetic, shards(): payload = term if payload is None else payload + term  7.18 us
    all_to_all x1, blocking collectives, shards(): lax.all_to_all(local_preds, 'block', split_axis=0, concat_axis=1, tiled=T...  7.01 us
  transfers between devices with their start and end apart: 1, of which 1 were waited for; matrix products, arithmetic and copies ran while one was open for 1% of the time, Pallas kernels for 0%

profile of v6, /device:TPU:0, one launch (start us, length us, event | category | flops | bytes accessed | tf_op | source)
XLA Modules:
  0.0 317.2 jit_solution(13910370170354365383)
XLA Ops:
  6.5 0.7 compare_select_fusion.5
  7.9 0.7 broadcast_multiply_fusion.1
  8.6 2.7 divide_convert_fusion
  12.2 1.0 broadcast_select_fusion.2
  27.6 7.2 %multiply_add_fusion = f32[16,1344,128]{2,1,0:T(8,128)} fusion(f32[1344,128]{1,0:T(8,128)S(1)} %get-tuple-element.33, f32[16]{0:T(128)S(1)} %get-tuple-element.57, f32[1344,128]{1,0:T(8,128)S(1)} %get-tuple-element.32, f32[16]{0:T(128)S(1)} %get-tuple-element.58, f32[1344,128]{1,0:T(8,128)S(1)} %get-tuple-element.31, f32[16]{0:T(128)S(1)} %get-tuple-element.59, ...), kind=kLoop, calls=%fused_computation.5 | loop fusion | flops 19267584 | bytes 13762816 | tf_op jit(solution)/shard_map/add | solution.py:208
  38.0 0.9 scatter_custom_fusion
  39.4 121.7 %reduce-scatter.2.cloned.1.call-done = f32[1,1344,128]{2,1,0:T(8,128)} async-done(((f32[16,1344,128]{2,1,0:T(8,128)}), f32[1,1344,128]{2,1,0:T(8,128)}) %reduce-scatter.2.cloned.1.call-update) | async-done | bytes 688144 | tf_op jit(solution)/shard_map/reduce_scatter | solution.py:211
  161.1 1.1 slice.411
  162.7 0.9 fusion.186
  163.6 22.0 %shard_map.109 = f32[2,128,128]{2,1,0:T(8,128)} custom-call(f32[2,128,128]{2,1,0:T(8,128)} %get-tuple-element.44.d_ref), custom_call_target="tpu_custom_call" | custom-call | flops 50331648 | bytes 262144 | tf_op jit(solution)/shard_map/pallas_call | solution.py:88
  185.7 0.7 broadcast_divide_fusion
  187.0 1.0 copy.59
  188.0 1.7 copy.48
  189.7 1.7 copy.49
  191.4 1.1 fusion.166
  192.4 1.4 fusion.43
  193.9 1.1 convolution_subtract_fusion
  196.8 22.0 %shard_map.110 = f32[2,128,128]{2,1,0:T(8,128)} custom-call(f32[2,128,128]{2,1,0:T(8,128)} %slice.424.d_ref), custom_call_target="tpu_custom_call" | custom-call | flops 50331648 | bytes 262144 | tf_op jit(solution)/shard_map/pallas_call | solution.py:88
  218.7 1.4 fusion.61
  220.1 1.2 fusion.164
  221.3 2.5 convolution_subtract_fusion.1
  224.1 1.6 slice.429.d_ref
  225.7 22.0 %shard_map.111 = f32[2,128,128]{2,1,0:T(8,128)} custom-call(f32[2,128,128]{2,1,0:T(8,128)} %slice.429.d_ref), custom_call_target="tpu_custom_call" | custom-call | flops 50331648 | bytes 262144 | tf_op jit(solution)/shard_map/pallas_call | solution.py:88
  247.7 1.4 fusion.131
  249.1 1.2 fusion.162
  250.3 2.0 convolution_subtract_fusion.2.d_ref
  252.6 22.0 %shard_map.112 = f32[2,128,128]{2,1,0:T(8,128)} custom-call(f32[2,128,128]{2,1,0:T(8,128)} %convolution_subtract_fusion.2.d_ref), custom_call_target="tpu_custom_call" | custom-call | flops 50331648 | bytes 262144 | tf_op jit(solution)/shard_map/pallas_call | solution.py:88
  274.6 1.2 fusion.190
  275.8 1.1 fusion.187
  278.5 21.2 %all_gather.3 = bf16[32,500,16]{1,2,0:T(8,128)(2,1)S(1)} all-gather(bf16[2,500,16]{1,2,0:T(8,128)(2,1)S(1)} %pad_maximum_fusion.9), channel_id=1, replica_groups=mesh['sample'=16,'block'=2] {'sample'}, dimensions={0}, use_global_device_ids=true | all-gather | bytes 544000 | tf_op jit(solution)/shard_map/all_gather | solution.py:241
  302.6 7.0 %all_to_all.18 = bf16[16,4,1024]{2,1,0:T(4,128)(2,1)S(1)} all-to-all(bf16[16,4,1024]{2,1,0:T(4,128)(2,1)S(1)} %pad_maximum_fusion.8), channel_id=1, replica_groups=mesh['sample'=16,'block'=2] {'block'}, dimensions={0} | all-to-all | bytes 262144 | tf_op jit(solution)/shard_map/all_to_all | solution.py:254
  309.7 0.7 all_to_all.16
  (176 shorter events, 26.3 us)
Async XLA Ops:
  6.5 5.1 %copy-start = (bf16[1024,16]{0,1:T(8,128)(2,1)S(1)}, bf16[1024,16]{0,1:T(8,128)(2,1)}, u32[]{:S(2)}) copy-start(bf16[1024,16]{0,1:T(8,128)(2,1)} %param.13) | copy-start | bytes 98308
  6.5 154.6 %reduce-scatter.2.cloned.1.call-start = ((), (), s32[]{:S(2)}) async-start(), calls=%async_computation.2 | async-start | bytes 11698176 | tf_op jit(solution)/shard_map/reduce_scatter | solution.py:211
  11.3 0.9 copy-start.13
  26.9 0.7 copy-start.16
  26.9 0.7 copy-start.15
  34.8 0.7 copy-start.17
  34.8 1.3 copy-start.1
  34.8 2.0 copy-start.2
  34.8 4.4 %copy-start.14 = (f32[10]{0:T(128)S(1)}, f32[10]{0:T(128)}, u32[]{:S(2)}) copy-start(f32[10]{0:T(128)} %constant.231) | copy-start | bytes 124
  162.6 22.9 %slice-start = ((f32[1,1344,128]{2,1,0:T(8,128)}), f32[1,64,128]{2,1,0:T(8,128)S(1)}, s32[]{:S(2)}) async-start(f32[1,1344,128]{2,1,0:T(8,128)} %reduce-scatter.2.cloned.1.call-done), calls=%async_computation.3 | async-start | bytes 65536 | tf_op jit(solution)/shard_map/slice | solution.py:215
  185.6 5.7 %copy-start.3 = (f32[2,128,128]{2,1,0:T(8,128)S(1)}, f32[2,128,128]{2,1,0:T(8,128)}, u32[]{:S(2)}) copy-start(f32[2,128,128]{2,1,0:T(8,128)} %shard_map.109) | copy-start | bytes 393220
  191.3 2.5 copy-start.7
  191.3 2.5 copy-start.8
  191.3 2.5 copy-start.9
  191.3 2.6 copy-start.10
  191.4 2.6 copy-start.11
  193.9 1.1 copy-start.12
  195.1 1.0 copy-start.6
  223.8 53.9 %copy-start.4 = (f32[2,128,128]{2,1,0:T(8,128)S(1)}, f32[2,128,128]{2,1,0:T(8,128)}, u32[]{:S(2)}) copy-start(f32[2,128,128]{2,1,0:T(8,128)} %shard_map.110) | copy-start | bytes 393220
  247.7 29.5 %copy-start.5 = (f32[2,128,128]{2,1,0:T(8,128)S(1)}, f32[2,128,128]{2,1,0:T(8,128)}, u32[]{:S(2)}) copy-start(f32[2,128,128]{2,1,0:T(8,128)} %shard_map.111) | copy-start | bytes 393220
Sparse Core Ops, SparseCore 0:
  34.9 126.1 reduce-scatter.1

commit v7 on v6

--- a/solution.py
+++ b/solution.py
@@ -64,23 +64,38 @@
     row_lane = lax.broadcasted_iota(jnp.int32, (1, n), 1)
     col_sub = lax.broadcasted_iota(jnp.int32, (n, 1), 0)
 
-    def step(j, carry):
+    def pick(row, k):
+        return jnp.sum(jnp.where(row_lane == k, row, 0.0), axis=1, keepdims=True)
+
+    def step(t, carry):
+        j = 2 * t
         for s in range(count):
             a = a_scr[s]
-            row = jnp.sum(jnp.where(sub == j, a, 0.0), axis=0, keepdims=True)
-            piv = jnp.sum(jnp.where(row_lane == j, row, 0.0), axis=1, keepdims=True)
-            scale = 1.0 / jnp.sqrt(piv)
-            col = jnp.sum(jnp.where(lane == j, a, 0.0), axis=1, keepdims=True)
-            lcol = jnp.where(col_sub >= j, col * scale, 0.0)
-            lrow = jnp.where(row_lane >= j, row * scale, 0.0)
-            a_scr[s] = a - lcol * lrow
+            row0 = jnp.sum(jnp.where(sub == j, a, 0.0), axis=0, keepdims=True)
+            row1 = jnp.sum(jnp.where(sub == j + 1, a, 0.0), axis=0, keepdims=True)
+            col0 = jnp.sum(jnp.where(lane == j, a, 0.0), axis=1, keepdims=True)
+            col1 = jnp.sum(jnp.where(lane == j + 1, a, 0.0), axis=1, keepdims=True)
+            top = jnp.sqrt(pick(row0, j))
+            inv_top = 1.0 / top
+            off = pick(row0, j + 1) * inv_top
+            bottom = jnp.sqrt(pick(row1, j + 1) - off * off)
+            inv_bottom = 1.0 / bottom
+            lcol0 = jnp.where(col_sub >= j, col0 * inv_top, 0.0)
+            lrow0 = jnp.where(row_lane >= j, row0 * inv_top, 0.0)
+            lcol1 = jnp.where(col_sub >= j + 1, (col1 - lcol0 * off) * inv_bottom, 0.0)
+            lrow1 = jnp.where(row_lane >= j + 1, (row1 - lrow0 * off) * inv_bottom, 0.0)
+            a_scr[s] = a - lcol0 * lrow0 - lcol1 * lrow1
             r = w_ref[s]
-            xrow = jnp.sum(jnp.where(sub == j, r, 0.0), axis=0, keepdims=True) * scale
-            strict = jnp.where(col_sub > j, lcol, 0.0)
-            w_ref[s] = jnp.where(sub == j, xrow, r - strict * xrow)
+            x0 = jnp.sum(jnp.where(sub == j, r, 0.0), axis=0, keepdims=True) * inv_top
+            w1 = jnp.sum(jnp.where(sub == j + 1, r, 0.0), axis=0, keepdims=True)
+            x1 = (w1 - off * x0) * inv_bottom
+            strict0 = jnp.where(col_sub > j + 1, lcol0, 0.0)
+            strict1 = jnp.where(col_sub > j + 1, lcol1, 0.0)
+            updated = r - strict0 * x0 - strict1 * x1
+            w_ref[s] = jnp.where(sub == j, x0, jnp.where(sub == j + 1, x1, updated))
         return carry
 
-    lax.fori_loop(0, n, step, 0)
+    lax.fori_loop(0, n // 2, step, 0)
 
 
 def inverse_factor(block):

time: 318 us -> 296 us (0.931)
  Pallas kernels: 88 us -> 65.6 us
    pallas_call x4, Pallas kernels: 88 us -> 65.6 us  [inverse_factor(): pl.pallas_call(inverse_factor_kernel, out_shape=jax.ShapeDtypeStruct(bloc...]
where the time goes in v7:
time: 296 us; the launch traced here: 295 us
  waiting for transfers between devices  122 us (41%)
  Pallas kernels  65.6 us (22%)
  matrix products  32.5 us (11%)
  blocking collectives  28.2 us (10%)
  other arithmetic  16.3 us (6%)
  local copies, waits for them, and re-layouts  15.6 us (5%)
  between operations  14.9 us (5%)
    reduce_scatter x1, waiting for transfers between devices, shards(): lax.psum_scatter(payload, 'sample', scatter_dimension=0, tiled=True)[0]  122 us
    pallas_call x4, Pallas kernels, inverse_factor(): pl.pallas_call(inverse_factor_kernel, out_shape=jax.ShapeDtypeStruct(bloc...  65.6 us
    all_gather x1, blocking collectives, shards(): collected = lax.all_gather(solved, 'sample', axis=0, tiled=True)  21.2 us
    dot_general x20, matrix products, mm(): jnp.einsum(spec, left, right, precision=HIGH, preferred_element_type=jnp....  18.3 us
    dot_general x56, matrix products, inner_products(): lax.dot_general(left_cols, right_cols, (((0,), (0,)), ((), ())), preferre...  12.8 us
    add x1, other arithmetic, shards(): payload = term if payload is None else payload + term  7.18 us
    all_to_all x1, blocking collectives, shards(): lax.all_to_all(local_preds, 'block', split_axis=0, concat_axis=1, tiled=T...  7 us
  transfers between devices with their start and end apart: 1, of which 1 were waited for; matrix products, arithmetic and copies ran while one was open for 1% of the time, Pallas kernels for 0%

profile of v7, /device:TPU:0, one launch (start us, length us, event | category | flops | bytes accessed | tf_op | source)
XLA Modules:
  0.0 294.8 jit_solution(1909326702911668256)
XLA Ops:
  6.5 0.7 compare_select_fusion.5
  7.9 0.7 broadcast_multiply_fusion.1
  8.6 2.7 divide_convert_fusion
  12.2 1.0 broadcast_select_fusion.2
  27.6 7.2 %multiply_add_fusion = f32[16,1344,128]{2,1,0:T(8,128)} fusion(f32[1344,128]{1,0:T(8,128)S(1)} %get-tuple-element.33, f32[16]{0:T(128)S(1)} %get-tuple-element.57, f32[1344,128]{1,0:T(8,128)S(1)} %get-tuple-element.32, f32[16]{0:T(128)S(1)} %get-tuple-element.58, f32[1344,128]{1,0:T(8,128)S(1)} %get-tuple-element.31, f32[16]{0:T(128)S(1)} %get-tuple-element.59, ...), kind=kLoop, calls=%fused_computation.5 | loop fusion | flops 19267584 | bytes 13762816 | tf_op jit(solution)/shard_map/add | solution.py:223
  38.0 0.9 scatter_custom_fusion
  39.4 121.7 %reduce-scatter.2.cloned.1.call-done = f32[1,1344,128]{2,1,0:T(8,128)} async-done(((f32[16,1344,128]{2,1,0:T(8,128)}), f32[1,1344,128]{2,1,0:T(8,128)}) %reduce-scatter.2.cloned.1.call-update) | async-done | bytes 688144 | tf_op jit(solution)/shard_map/reduce_scatter | solution.py:226
  161.1 1.1 slice.411
  162.7 0.9 fusion.186
  163.6 16.4 %shard_map.109 = f32[2,128,128]{2,1,0:T(8,128)} custom-call(f32[2,128,128]{2,1,0:T(8,128)} %get-tuple-element.44.d_ref), custom_call_target="tpu_custom_call" | custom-call | flops 50331648 | bytes 262144 | tf_op jit(solution)/shard_map/pallas_call | solution.py:103
  180.1 0.7 broadcast_divide_fusion
  181.4 1.0 copy.59
  182.4 1.7 copy.48
  184.1 1.7 copy.49
  185.8 1.1 fusion.166
  186.9 1.4 fusion.43
  188.3 1.1 convolution_subtract_fusion
  191.2 16.4 %shard_map.110 = f32[2,128,128]{2,1,0:T(8,128)} custom-call(f32[2,128,128]{2,1,0:T(8,128)} %slice.424.d_ref), custom_call_target="tpu_custom_call" | custom-call | flops 50331648 | bytes 262144 | tf_op jit(solution)/shard_map/pallas_call | solution.py:103
  207.6 1.4 fusion.61
  208.9 1.2 fusion.164
  210.1 2.5 convolution_subtract_fusion.1
  212.9 1.6 slice.429.d_ref
  214.5 16.4 %shard_map.111 = f32[2,128,128]{2,1,0:T(8,128)} custom-call(f32[2,128,128]{2,1,0:T(8,128)} %slice.429.d_ref), custom_call_target="tpu_custom_call" | custom-call | flops 50331648 | bytes 262144 | tf_op jit(solution)/shard_map/pallas_call | solution.py:103
  230.9 1.4 fusion.131
  232.3 1.2 fusion.162
  233.5 2.0 convolution_subtract_fusion.2.d_ref
  235.8 16.4 %shard_map.112 = f32[2,128,128]{2,1,0:T(8,128)} custom-call(f32[2,128,128]{2,1,0:T(8,128)} %convolution_subtract_fusion.2.d_ref), custom_call_target="tpu_custom_call" | custom-call | flops 50331648 | bytes 262144 | tf_op jit(solution)/shard_map/pallas_call | solution.py:103
  252.2 1.2 fusion.190
  253.4 1.1 fusion.187
  256.1 21.2 %all_gather.3 = bf16[32,500,16]{1,2,0:T(8,128)(2,1)S(1)} all-gather(bf16[2,500,16]{1,2,0:T(8,128)(2,1)S(1)} %pad_maximum_fusion.9), channel_id=1, replica_groups=mesh['sample'=16,'block'=2] {'sample'}, dimensions={0}, use_global_device_ids=true | all-gather | bytes 544000 | tf_op jit(solution)/shard_map/all_gather | solution.py:256
  280.2 7.0 %all_to_all.18 = bf16[16,4,1024]{2,1,0:T(4,128)(2,1)S(1)} all-to-all(bf16[16,4,1024]{2,1,0:T(4,128)(2,1)S(1)} %pad_maximum_fusion.8), channel_id=1, replica_groups=mesh['sample'=16,'block'=2] {'block'}, dimensions={0} | all-to-all | bytes 262144 | tf_op jit(solution)/shard_map/all_to_all | solution.py:269
  287.3 0.7 all_to_all.16
  (176 shorter events, 26.3 us)
Async XLA Ops:
  6.5 5.1 %copy-start = (bf16[1024,16]{0,1:T(8,128)(2,1)S(1)}, bf16[1024,16]{0,1:T(8,128)(2,1)}, u32[]{:S(2)}) copy-start(bf16[1024,16]{0,1:T(8,128)(2,1)} %param.13) | copy-start | bytes 98308
  6.5 154.6 %reduce-scatter.2.cloned.1.call-start = ((), (), s32[]{:S(2)}) async-start(), calls=%async_computation.2 | async-start | bytes 11698176 | tf_op jit(solution)/shard_map/reduce_scatter | solution.py:226
  11.3 0.9 copy-start.13
  26.9 0.7 copy-start.16
  26.9 0.7 copy-start.15
  34.8 0.7 copy-start.17
  34.8 1.3 copy-start.1
  34.8 2.0 copy-start.2
  34.8 4.4 %copy-start.14 = (f32[10]{0:T(128)S(1)}, f32[10]{0:T(128)}, u32[]{:S(2)}) copy-start(f32[10]{0:T(128)} %constant.231) | copy-start | bytes 124
  162.6 17.4 %slice-start = ((f32[1,1344,128]{2,1,0:T(8,128)}), f32[1,64,128]{2,1,0:T(8,128)S(1)}, s32[]{:S(2)}) async-start(f32[1,1344,128]{2,1,0:T(8,128)} %reduce-scatter.2.cloned.1.call-done), calls=%async_computation.3 | async-start | bytes 65536 | tf_op jit(solution)/shard_map/slice | solution.py:230
  180.0 5.7 %copy-start.3 = (f32[2,128,128]{2,1,0:T(8,128)S(1)}, f32[2,128,128]{2,1,0:T(8,128)}, u32[]{:S(2)}) copy-start(f32[2,128,128]{2,1,0:T(8,128)} %shard_map.109) | copy-start | bytes 393220
  185.7 2.5 copy-start.7
  185.7 2.5 copy-start.8
  185.7 2.5 copy-start.9
  185.8 2.6 copy-start.10
  185.8 2.6 copy-start.11
  188.3 1.1 copy-start.12
  189.5 1.0 copy-start.6
  212.6 42.7 %copy-start.4 = (f32[2,128,128]{2,1,0:T(8,128)S(1)}, f32[2,128,128]{2,1,0:T(8,128)}, u32[]{:S(2)}) copy-start(f32[2,128,128]{2,1,0:T(8,128)} %shard_map.110) | copy-start | bytes 393220
  230.9 23.9 %copy-start.5 = (f32[2,128,128]{2,1,0:T(8,128)S(1)}, f32[2,128,128]{2,1,0:T(8,128)}, u32[]{:S(2)}) copy-start(f32[2,128,128]{2,1,0:T(8,128)} %shard_map.111) | copy-start | bytes 393220
Sparse Core Ops, SparseCore 0:
  34.9 126.1 reduce-scatter.1

commit v8 on v7

--- a/solution.py
+++ b/solution.py
@@ -147,6 +147,53 @@
     return solved
 
 
+def pack_tiles(tiles, panels):
+    pairs = tile_pairs(panels)
+    off = [tiles[index] for index, (r, c) in enumerate(pairs) if r < c]
+    diag = [tiles[pairs.index((p, p))] for p in range(panels)]
+    sub = lax.broadcasted_iota(jnp.int32, (PANEL, PANEL), 0)
+    lane = lax.broadcasted_iota(jnp.int32, (PANEL, PANEL), 1)
+    packed = []
+    spare = []
+    for p in range(0, panels - 1, 2):
+        packed.append(jnp.where(sub <= lane, diag[p], diag[p + 1]))
+        spare.append(jnp.sum(jnp.where(sub == lane, diag[p + 1], 0.0), axis=0))
+    if panels % 2:
+        packed.append(diag[panels - 1])
+    spare_rows = jnp.zeros((8, PANEL), jnp.float32)
+    if spare:
+        spare_rows = spare_rows.at[: len(spare)].set(jnp.stack(spare))
+    return jnp.concatenate([jnp.stack(off + packed).reshape(-1, PANEL), spare_rows])
+
+
+def unpack_tiles(rows, panels):
+    pairs = tile_pairs(panels)
+    span = rows.shape[0]
+    off_count = len(pairs) - panels
+    packed_count = (panels + 1) // 2
+    body = rows[:, : (off_count + packed_count) * PANEL].reshape(span, off_count + packed_count, PANEL, PANEL)
+    spare = rows[:, (off_count + packed_count) * PANEL :]
+    sub = lax.broadcasted_iota(jnp.int32, (PANEL, PANEL), 0)
+    lane = lax.broadcasted_iota(jnp.int32, (PANEL, PANEL), 1)
+    diag = []
+    for index in range(packed_count):
+        tile = body[:, off_count + index]
+        flipped = jnp.swapaxes(tile, 1, 2)
+        diag.append(jnp.where(sub <= lane, tile, flipped))
+        if 2 * index + 1 < panels:
+            lower = jnp.where(sub > lane, tile, flipped)
+            diag.append(jnp.where(sub == lane, spare[:, index][:, None, :], lower))
+    out = []
+    off_index = 0
+    for r, c in pairs:
+        if r == c:
+            out.append(diag[r])
+        else:
+            out.append(body[:, off_index])
+            off_index += 1
+    return jnp.stack(out, axis=1)
+
+
 def owned_layout(systems, devices, ridge_count):
     share = -(-systems // devices)
     firsts = []
@@ -194,7 +241,7 @@
         for member in range(member_count):
             columns = jnp.pad(column_sets[member], ((0, 0), (0, padded_width - SNPS)))
             masked = jnp.where(slot_masks[slot][:, None], columns, jnp.zeros_like(columns))
-            tiles = tile_grams(masked, columns, panels)
+            tiles = pack_tiles(tile_grams(masked, columns, panels), panels)
             cross = jnp.stack(
                 [inner_products(ordered, masked[:, p * PANEL : (p + 1) * PANEL]) for p in range(panels)]
             )
@@ -225,8 +272,8 @@
     payload = payload.reshape(devices, span * row_count, PANEL)
     reduced = lax.psum_scatter(payload, "sample", scatter_dimension=0, tiled=True)[0]
     reduced = reduced.reshape(span, row_count, PANEL)
-    split = tile_count * PANEL
-    mine_grams = reduced[:, :split].reshape(span, tile_count, PANEL, PANEL)
+    split = row_count - panels * traits
+    mine_grams = unpack_tiles(reduced[:, :split], panels)
     mine_crosses = reduced[:, split:].reshape(span, panels, traits, PANEL)
 
     owned_ids = jnp.minimum(me * share + lax.broadcasted_iota(jnp.int32, (share,), 0), systems - 1)

time: 296 us -> 361 us (1.22)
  waiting for transfers between devices: 122 us -> 176 us
  matrix products: 32.5 us -> 39 us
  local copies, waits for them, and re-layouts: 15.6 us -> 20.5 us
    unnamed x1 -> x2, waiting for transfers between devices: 0.02 us -> 176 us
    reduce_scatter x1 -> x0, waiting for transfers between devices: 122 us -> none  [shards(): lax.psum_scatter(payload, 'sample', scatter_dimension=0, tiled=True)[0]]
    dot_general x56, matrix products: 12.8 us -> 19.4 us  [inner_products(): lax.dot_general(left_cols, right_cols, (((0,), (0,)), ((), ())), preferre...]
where the time goes in v8:
time: 361 us; the launch traced here: 360 us
  waiting for transfers between devices  176 us (49%)
  Pallas kernels  65.6 us (18%)
  matrix products  39 us (11%)
  blocking collectives  28.7 us (8%)
  local copies, waits for them, and re-layouts  20.5 us (6%)
  other arithmetic  15.2 us (4%)
  between operations  15 us (4%)
    unnamed x2, waiting for transfers between devices  176 us
    pallas_call x4, Pallas kernels, inverse_factor(): pl.pallas_call(inverse_factor_kernel, out_shape=jax.ShapeDtypeStruct(bloc...  65.6 us
    all_gather x1, blocking collectives, shards(): collected = lax.all_gather(solved, 'sample', axis=0, tiled=True)  21.7 us
    dot_general x56, matrix products, inner_products(): lax.dot_general(left_cols, right_cols, (((0,), (0,)), ((), ())), preferre...  19.4 us
    dot_general x20, matrix products, mm(): jnp.einsum(spec, left, right, precision=HIGH, preferred_element_type=jnp....  18.2 us
  transfers between devices with their start and end apart: 1, of which 1 were waited for; matrix products, arithmetic and copies ran while one was open for 1% of the time, Pallas kernels for 0%

profile of v8, /device:TPU:0, one launch (start us, length us, event | category | flops | bytes accessed | tf_op | source)
XLA Modules:
  0.0 360.3 jit_solution(18417552862058272987)
XLA Ops:
  7.2 2.7 divide_convert_fusion
  10.6 2.4 broadcast_select_fusion.2
  13.0 1.1 fusion.40
  15.9 1.2 convolution_bitcast_fusion.36
  17.2 1.2 convolution_bitcast_fusion.37
  18.4 1.2 convolution_bitcast_fusion.38
  19.5 1.2 convolution_bitcast_fusion.39
  20.7 1.2 fusion.30
  34.8 5.9 %multiply_add_fusion = f32[16,1096,128]{2,1,0:T(8,128)} fusion(f32[1096,128]{1,0:T(8,128)S(1)} %get-tuple-element.94, f32[16]{0:T(128)S(1)} %get-tuple-element.109, f32[1096,128]{1,0:T(8,128)S(1)} %get-tuple-element.93, f32[16]{0:T(128)S(1)} %get-tuple-element.110, f32[1096,128]{1,0:T(8,128)S(1)} %get-tuple-element.92, f32[16]{0:T(128)S(1)} %get-tuple-element.111, ...), kind=kLoop, calls=%fused_computation.5 | loop fusion | flops 15712256 | bytes 11223296 | tf_op jit(solution)/shard_map/add | solution.py:270
  46.0 176.2 %all-reduce.8.cloned.1.call-done = f32[16,1096,128]{2,1,0:T(8,128)} async-done(((f32[16,1096,128]{2,1,0:T(8,128)}), f32[16,1096,128]{2,1,0:T(8,128)}) %all-reduce.8.cloned.1.call-update) | async-done | bytes 8978448
  222.3 1.7 constant_dynamic-slice_fusion.2
  224.2 1.4 fusion.189
  227.1 16.4 %shard_map.109 = f32[2,128,128]{2,1,0:T(8,128)} custom-call(f32[2,128,128]{2,1,0:T(8,128)} %get-tuple-element.90.d_ref), custom_call_target="tpu_custom_call" | custom-call | flops 50331648 | bytes 262144 | tf_op jit(solution)/shard_map/pallas_call | solution.py:103
  243.5 1.4 constant_dynamic-slice_fusion.3
  247.4 1.7 copy.56
  249.0 1.7 copy.57
  251.8 1.4 fusion.43
  253.3 1.1 convolution_subtract_fusion
  256.1 16.4 %shard_map.110 = f32[2,128,128]{2,1,0:T(8,128)} custom-call(f32[2,128,128]{2,1,0:T(8,128)} %slice.530.d_ref), custom_call_target="tpu_custom_call" | custom-call | flops 50331648 | bytes 262144 | tf_op jit(solution)/shard_map/pallas_call | solution.py:103
  272.5 1.4 fusion.61
  273.9 1.2 fusion.174
  275.1 2.4 convolution_subtract_fusion.1
  277.9 1.6 slice.535.d_ref
  279.4 16.4 %shard_map.111 = f32[2,128,128]{2,1,0:T(8,128)} custom-call(f32[2,128,128]{2,1,0:T(8,128)} %slice.535.d_ref), custom_call_target="tpu_custom_call" | custom-call | flops 50331648 | bytes 262144 | tf_op jit(solution)/shard_map/pallas_call | solution.py:103
  295.8 1.4 fusion.139
  297.2 1.2 fusion.172
  298.4 2.0 convolution_subtract_fusion.2.d_ref
  300.7 16.4 %shard_map.112 = f32[2,128,128]{2,1,0:T(8,128)} custom-call(f32[2,128,128]{2,1,0:T(8,128)} %convolution_subtract_fusion.2.d_ref), custom_call_target="tpu_custom_call" | custom-call | flops 50331648 | bytes 262144 | tf_op jit(solution)/shard_map/pallas_call | solution.py:103
  317.1 1.2 fusion.202
  318.3 1.1 fusion.199
  321.1 21.7 %all_gather.3 = bf16[32,500,16]{1,2,0:T(8,128)(2,1)S(1)} all-gather(bf16[2,500,16]{1,2,0:T(8,128)(2,1)S(1)} %pad_maximum_fusion.9), channel_id=1, replica_groups=mesh['sample'=16,'block'=2] {'sample'}, dimensions={0}, use_global_device_ids=true | all-gather | bytes 544000 | tf_op jit(solution)/shard_map/all_gather | solution.py:303
  345.7 7.0 %all_to_all.18 = bf16[16,4,1024]{2,1,0:T(4,128)(2,1)S(1)} all-to-all(bf16[16,4,1024]{2,1,0:T(4,128)(2,1)S(1)} %pad_maximum_fusion.8), channel_id=1, replica_groups=mesh['sample'=16,'block'=2] {'block'}, dimensions={0} | all-to-all | bytes 262144 | tf_op jit(solution)/shard_map/all_to_all | solution.py:316
  (213 shorter events, 32.6 us)
Async XLA Ops:
  6.5 8.8 %copy-start = (bf16[1024,16]{0,1:T(8,128)(2,1)S(1)}, bf16[1024,16]{0,1:T(8,128)(2,1)}, u32[]{:S(2)}) copy-start(bf16[1024,16]{0,1:T(8,128)(2,1)} %param.21) | copy-start | bytes 98308
  6.5 215.7 %all-reduce.8.cloned.1.call-start = ((), (), s32[]{:S(2)}) async-start(), calls=%async_computation.1 | async-start | bytes 17956864
  10.0 0.7 copy-start.21
  13.0 2.3 copy-start.8
  13.0 2.3 copy-start.11
  13.0 2.2 copy-start.25
  15.9 6.0 %copy-start.4 = (bf16[1024,512]{0,1:T(8,128)(2,1)S(1)}, bf16[1024,512]{0,1:T(8,128)(2,1)}, u32[]{:S(2)}) copy-start(bf16[1024,512]{0,1:T(8,128)(2,1)} %get-tuple-element.95) | copy-start | bytes 3145732
  21.9 1.4 copy-start.9
  21.9 1.5 copy-start.10
  22.9 2.2 copy-start.3
  25.4 1.4 copy-start.12
  25.4 1.4 copy-start.16
  28.5 0.8 copy-start.28
  34.1 0.7 copy-start.24
  34.2 0.7 copy-start.23
  40.8 0.7 copy-start.27
  40.8 1.3 copy-start.26
  40.8 2.0 copy-start.1
  40.8 2.6 copy-start.2
  40.8 5.1 %copy-start.22 = (f32[10]{0:T(128)S(1)}, f32[10]{0:T(128)}, u32[]{:S(2)}) copy-start(f32[10]{0:T(128)} %constant.324) | copy-start | bytes 124
  245.0 5.7 %copy-start.5 = (f32[2,128,128]{2,1,0:T(8,128)S(1)}, f32[2,128,128]{2,1,0:T(8,128)}, u32[]{:S(2)}) copy-start(f32[2,128,128]{2,1,0:T(8,128)} %shard_map.109) | copy-start | bytes 393220
  250.7 2.5 copy-start.14
  250.7 2.5 copy-start.15
  250.7 2.5 copy-start.17
  250.7 2.6 copy-start.18
  250.7 2.6 copy-start.19
  253.3 1.1 copy-start.20
  254.4 1.0 copy-start.13
  277.5 42.7 %copy-start.6 = (f32[2,128,128]{2,1,0:T(8,128)S(1)}, f32[2,128,128]{2,1,0:T(8,128)}, u32[]{:S(2)}) copy-start(f32[2,128,128]{2,1,0:T(8,128)} %shard_map.110) | copy-start | bytes 393220
  295.8 23.9 %copy-start.7 = (f32[2,128,128]{2,1,0:T(8,128)S(1)}, f32[2,128,128]{2,1,0:T(8,128)}, u32[]{:S(2)}) copy-start(f32[2,128,128]{2,1,0:T(8,128)} %shard_map.111) | copy-start | bytes 393220
Sparse Core Ops, SparseCore 0:
  41.0 181.2 all-reduce.7

commit v9 on v8

--- a/solution.py
+++ b/solution.py
@@ -8,6 +8,7 @@
 SNPS = 500
 FOLDS = 5
 PANEL = 128
+ROW_ALIGN = 16
 HIGH = lax.Precision.HIGHEST
 
 
@@ -242,10 +243,13 @@
             columns = jnp.pad(column_sets[member], ((0, 0), (0, padded_width - SNPS)))
             masked = jnp.where(slot_masks[slot][:, None], columns, jnp.zeros_like(columns))
             tiles = pack_tiles(tile_grams(masked, columns, panels), panels)
+            tiles_rows = tiles.shape[0]
             cross = jnp.stack(
                 [inner_products(ordered, masked[:, p * PANEL : (p + 1) * PANEL]) for p in range(panels)]
             )
-            member_rows.append(jnp.concatenate([tiles.reshape(-1, PANEL), cross.reshape(-1, PANEL)]))
+            joined = jnp.concatenate([tiles.reshape(-1, PANEL), cross.reshape(-1, PANEL)])
+            joined = jnp.pad(joined, ((0, -joined.shape[0] % ROW_ALIGN), (0, 0)))
+            member_rows.append(joined)
         slot_rows.append(jnp.stack(member_rows))
     local_rows = jnp.stack(slot_rows)
 
@@ -272,9 +276,9 @@
     payload = payload.reshape(devices, span * row_count, PANEL)
     reduced = lax.psum_scatter(payload, "sample", scatter_dimension=0, tiled=True)[0]
     reduced = reduced.reshape(span, row_count, PANEL)
-    split = row_count - panels * traits
-    mine_grams = unpack_tiles(reduced[:, :split], panels)
-    mine_crosses = reduced[:, split:].reshape(span, panels, traits, PANEL)
+    crosses_at = tiles_rows
+    mine_grams = unpack_tiles(reduced[:, :crosses_at], panels)
+    mine_crosses = reduced[:, crosses_at : crosses_at + panels * traits].reshape(span, panels, traits, PANEL)
 
     owned_ids = jnp.minimum(me * share + lax.broadcasted_iota(jnp.int32, (share,), 0), systems - 1)
     pair_ids = owned_ids // ridge_count

time: 361 us -> 292 us (0.81)
  waiting for transfers between devices: 176 us -> 107 us
  other arithmetic: 15.2 us -> 19.1 us
    unnamed x2 -> x1, waiting for transfers between devices: 176 us -> 0.02 us
    reduce_scatter x0 -> x1, waiting for transfers between devices: none -> 107 us  [shards(): lax.psum_scatter(payload, 'sample', scatter_dimension=0, tiled=True)[0]]
where the time goes in v9:
time: 292 us; the launch traced here: 291 us
  waiting for transfers between devices  107 us (37%)
  Pallas kernels  65.6 us (22%)
  matrix products  38.4 us (13%)
  blocking collectives  28.5 us (10%)
  other arithmetic  19.1 us (7%)
  local copies, waits for them, and re-layouts  17 us (6%)
  between operations  14.9 us (5%)
    reduce_scatter x1, waiting for transfers between devices, shards(): lax.psum_scatter(payload, 'sample', scatter_dimension=0, tiled=True)[0]  107 us
    pallas_call x4, Pallas kernels, inverse_factor(): pl.pallas_call(inverse_factor_kernel, out_shape=jax.ShapeDtypeStruct(bloc...  65.6 us
    all_gather x1, blocking collectives, shards(): collected = lax.all_gather(solved, 'sample', axis=0, tiled=True)  21.5 us
    dot_general x56, matrix products, inner_products(): lax.dot_general(left_cols, right_cols, (((0,), (0,)), ((), ())), preferre...  19.4 us
    dot_general x20, matrix products, mm(): jnp.einsum(spec, left, right, precision=HIGH, preferred_element_type=jnp....  17.7 us
    all_to_all x1, blocking collectives, shards(): lax.all_to_all(local_preds, 'block', split_axis=0, concat_axis=1, tiled=T...  7.03 us
    unnamed x55, local copies, waits for them, and re-layouts  6.01 us
    add x1, other arithmetic, shards(): payload = term if payload is None else payload + term  5.97 us
  transfers between devices with their start and end apart: 1, of which 1 were waited for; matrix products, arithmetic and copies ran while one was open for 1% of the time, Pallas kernels for 0%

profile of v9, /device:TPU:0, one launch (start us, length us, event | category | flops | bytes accessed | tf_op | source)
XLA Modules:
  0.0 290.7 jit_solution(10046359520266712975)
XLA Ops:
  7.2 2.7 divide_convert_fusion
  10.6 2.4 broadcast_select_fusion.2
  13.0 1.1 fusion.40
  15.9 1.2 convolution_bitcast_fusion.36
  17.1 1.2 convolution_bitcast_fusion.37
  18.3 1.2 convolution_bitcast_fusion.38
  19.5 1.2 convolution_bitcast_fusion.39
  20.7 1.2 fusion.30
  34.8 6.0 %multiply_add_fusion = f32[16,1104,128]{2,1,0:T(8,128)} fusion(f32[1104,128]{1,0:T(8,128)S(1)} %get-tuple-element.92, f32[16]{0:T(128)S(1)} %get-tuple-element.109, f32[1104,128]{1,0:T(8,128)S(1)} %get-tuple-element.91, f32[16]{0:T(128)S(1)} %get-tuple-element.110, f32[1104,128]{1,0:T(8,128)S(1)} %get-tuple-element.90, f32[16]{0:T(128)S(1)} %get-tuple-element.111, ...), kind=kLoop, calls=%fused_computation.5 | loop fusion | flops 15826944 | bytes 11305216 | tf_op jit(solution)/shard_map/add | solution.py:274
  45.2 107.1 %reduce-scatter.2.cloned.1.call-done = f32[1,1104,128]{2,1,0:T(8,128)} async-done(((f32[16,1104,128]{2,1,0:T(8,128)}), f32[1,1104,128]{2,1,0:T(8,128)}) %reduce-scatter.2.cloned.1.call-update) | async-done | bytes 565264 | tf_op jit(solution)/shard_map/reduce_scatter | solution.py:277
  152.4 1.1 slice.514
  159.0 1.5 multiply_add_fusion.1
  161.4 16.4 %shard_map.109 = f32[2,128,128]{2,1,0:T(8,128)} custom-call(f32[2,128,128]{2,1,0:T(8,128)} %get-tuple-element.88.d_ref), custom_call_target="tpu_custom_call" | custom-call | flops 50331648 | bytes 262144 | tf_op jit(solution)/shard_map/pallas_call | solution.py:104
  178.3 0.9 pad_maximum_fusion.7
  179.3 1.0 copy.58
  180.3 1.0 copy.67
  181.4 1.0 copy.57
  182.7 1.4 fusion.47
  184.1 2.1 convolution_subtract_fusion
  187.9 16.4 %shard_map.110 = f32[2,128,128]{2,1,0:T(8,128)} custom-call(f32[2,128,128]{2,1,0:T(8,128)} %slice.534.d_ref), custom_call_target="tpu_custom_call" | custom-call | flops 50331648 | bytes 262144 | tf_op jit(solution)/shard_map/pallas_call | solution.py:104
  204.3 1.4 fusion.65
  205.7 1.2 fusion.178
  206.9 1.7 convolution_subtract_fusion.1
  210.1 16.4 %shard_map.111 = f32[2,128,128]{2,1,0:T(8,128)} custom-call(f32[2,128,128]{2,1,0:T(8,128)} %slice.539.d_ref), custom_call_target="tpu_custom_call" | custom-call | flops 50331648 | bytes 262144 | tf_op jit(solution)/shard_map/pallas_call | solution.py:104
  226.5 1.4 fusion.143
  227.9 1.2 fusion.176
  229.1 2.0 convolution_subtract_fusion.2.d_ref
  231.4 16.4 %shard_map.112 = f32[2,128,128]{2,1,0:T(8,128)} custom-call(f32[2,128,128]{2,1,0:T(8,128)} %convolution_subtract_fusion.2.d_ref), custom_call_target="tpu_custom_call" | custom-call | flops 50331648 | bytes 262144 | tf_op jit(solution)/shard_map/pallas_call | solution.py:104
  247.8 1.2 fusion.204
  249.0 1.1 fusion.201
  251.7 21.5 %all_gather.3 = bf16[32,500,16]{1,2,0:T(8,128)(2,1)S(1)} all-gather(bf16[2,500,16]{1,2,0:T(8,128)(2,1)S(1)} %pad_maximum_fusion.9), channel_id=1, replica_groups=mesh['sample'=16,'block'=2] {'sample'}, dimensions={0}, use_global_device_ids=true | all-gather | bytes 544000 | tf_op jit(solution)/shard_map/all_gather | solution.py:307
  276.1 7.0 %all_to_all.18 = bf16[16,4,1024]{2,1,0:T(4,128)(2,1)S(1)} all-to-all(bf16[16,4,1024]{2,1,0:T(4,128)(2,1)S(1)} %pad_maximum_fusion.8), channel_id=1, replica_groups=mesh['sample'=16,'block'=2] {'block'}, dimensions={0} | all-to-all | bytes 262144 | tf_op jit(solution)/shard_map/all_to_all | solution.py:320
  (203 shorter events, 35.2 us)
Async XLA Ops:
  6.5 8.7 %copy-start = (bf16[1024,16]{0,1:T(8,128)(2,1)S(1)}, bf16[1024,16]{0,1:T(8,128)(2,1)}, u32[]{:S(2)}) copy-start(bf16[1024,16]{0,1:T(8,128)(2,1)} %param.21) | copy-start | bytes 98308
  6.5 145.9 %reduce-scatter.2.cloned.1.call-start = ((), (), s32[]{:S(2)}) async-start(), calls=%async_computation.2 | async-start | bytes 9609216 | tf_op jit(solution)/shard_map/reduce_scatter | solution.py:277
  10.0 0.7 copy-start.17
  13.0 2.2 copy-start.10
  13.0 2.3 copy-start.13
  13.0 2.2 copy-start.21
  15.9 6.0 %copy-start.4 = (bf16[1024,512]{0,1:T(8,128)(2,1)S(1)}, bf16[1024,512]{0,1:T(8,128)(2,1)}, u32[]{:S(2)}) copy-start(bf16[1024,512]{0,1:T(8,128)(2,1)} %get-tuple-element.93) | copy-start | bytes 3145732
  21.9 1.4 copy-start.11
  21.9 1.5 copy-start.12
  22.8 2.2 copy-start.3
  25.3 1.4 copy-start.14
  25.3 1.4 copy-start.16
  28.4 0.8 copy-start.23
  34.1 0.7 copy-start.20
  34.1 0.7 copy-start.19
  40.8 0.7 copy-start.22
  40.8 1.3 copy-start.1
  40.8 1.9 copy-start.2
  40.8 4.3 %copy-start.18 = (f32[10]{0:T(128)S(1)}, f32[10]{0:T(128)}, u32[]{:S(2)}) copy-start(f32[10]{0:T(128)} %constant.333) | copy-start | bytes 124
  160.5 17.3 %slice-start = ((f32[1,1104,128]{2,1,0:T(8,128)}), f32[1,64,128]{2,1,0:T(8,128)S(1)}, s32[]{:S(2)}) async-start(f32[1,1104,128]{2,1,0:T(8,128)} %reduce-scatter.2.cloned.1.call-done), calls=%async_computation.3 | async-start | bytes 65536 | tf_op jit(solution)/shard_map/slice | solution.py:281
  177.8 4.6 %copy-start.5 = (f32[2,128,128]{2,1,0:T(8,128)S(1)}, f32[2,128,128]{2,1,0:T(8,128)}, u32[]{:S(2)}) copy-start(f32[2,128,128]{2,1,0:T(8,128)} %shard_map.109) | copy-start | bytes 393220
  182.4 1.7 copy-start.8
  186.2 1.1 copy-start.15
  208.6 0.8 copy-start.9
  208.6 42.3 %copy-start.6 = (f32[2,128,128]{2,1,0:T(8,128)S(1)}, f32[2,128,128]{2,1,0:T(8,128)}, u32[]{:S(2)}) copy-start(f32[2,128,128]{2,1,0:T(8,128)} %shard_map.110) | copy-start | bytes 393220
  226.5 23.9 %copy-start.7 = (f32[2,128,128]{2,1,0:T(8,128)S(1)}, f32[2,128,128]{2,1,0:T(8,128)}, u32[]{:S(2)}) copy-start(f32[2,128,128]{2,1,0:T(8,128)} %shard_map.111) | copy-start | bytes 393220
Sparse Core Ops, SparseCore 0:
  40.9 111.4 reduce-scatter.1

commit v10 on v9

--- a/solution.py
+++ b/solution.py
@@ -96,7 +96,7 @@
             w_ref[s] = jnp.where(sub == j, x0, jnp.where(sub == j + 1, x1, updated))
         return carry
 
-    lax.fori_loop(0, n // 2, step, 0)
+    lax.fori_loop(0, n // 2, step, 0, unroll=4)
 
 
 def inverse_factor(block):

time: 292 us -> 289 us (0.990)
  no operation moved by 1% of the time
where the time goes in v10:
time: 289 us; the launch traced here: 288 us
  waiting for transfers between devices  107 us (37%)
  Pallas kernels  63.2 us (22%)
  matrix products  38.4 us (13%)
  blocking collectives  28.5 us (10%)
  other arithmetic  19.1 us (7%)
  local copies, waits for them, and re-layouts  17 us (6%)
  between operations  14.9 us (5%)
    reduce_scatter x1, waiting for transfers between devices, shards(): lax.psum_scatter(payload, 'sample', scatter_dimension=0, tiled=True)[0]  107 us
    pallas_call x4, Pallas kernels, inverse_factor(): pl.pallas_call(inverse_factor_kernel, out_shape=jax.ShapeDtypeStruct(bloc...  63.2 us
    all_gather x1, blocking collectives, shards(): collected = lax.all_gather(solved, 'sample', axis=0, tiled=True)  21.5 us
    dot_general x56, matrix products, inner_products(): lax.dot_general(left_cols, right_cols, (((0,), (0,)), ((), ())), preferre...  19.4 us
    dot_general x20, matrix products, mm(): jnp.einsum(spec, left, right, precision=HIGH, preferred_element_type=jnp....  17.7 us
    all_to_all x1, blocking collectives, shards(): lax.all_to_all(local_preds, 'block', split_axis=0, concat_axis=1, tiled=T...  7.04 us
    unnamed x55, local copies, waits for them, and re-layouts  6.01 us
    add x1, other arithmetic, shards(): payload = term if payload is None else payload + term  5.97 us
  transfers between devices with their start and end apart: 1, of which 1 were waited for; matrix products, arithmetic and copies ran while one was open for 1% of the time, Pallas kernels for 0%

profile of v10, /device:TPU:0, one launch (start us, length us, event | category | flops | bytes accessed | tf_op | source)
XLA Modules:
  0.0 288.3 jit_solution(4276766451190765689)
XLA Ops:
  7.2 2.7 divide_convert_fusion
  10.6 2.4 broadcast_select_fusion.2
  13.0 1.1 fusion.40
  15.9 1.2 convolution_bitcast_fusion.36
  17.1 1.2 convolution_bitcast_fusion.37
  18.3 1.2 convolution_bitcast_fusion.38
  19.5 1.2 convolution_bitcast_fusion.39
  20.7 1.2 fusion.30
  34.8 6.0 %multiply_add_fusion = f32[16,1104,128]{2,1,0:T(8,128)} fusion(f32[1104,128]{1,0:T(8,128)S(1)} %get-tuple-element.92, f32[16]{0:T(128)S(1)} %get-tuple-element.109, f32[1104,128]{1,0:T(8,128)S(1)} %get-tuple-element.91, f32[16]{0:T(128)S(1)} %get-tuple-element.110, f32[1104,128]{1,0:T(8,128)S(1)} %get-tuple-element.90, f32[16]{0:T(128)S(1)} %get-tuple-element.111, ...), kind=kLoop, calls=%fused_computation.5 | loop fusion | flops 15826944 | bytes 11305216 | tf_op jit(solution)/shard_map/add | solution.py:274
  45.2 107.1 %reduce-scatter.2.cloned.1.call-done = f32[1,1104,128]{2,1,0:T(8,128)} async-done(((f32[16,1104,128]{2,1,0:T(8,128)}), f32[1,1104,128]{2,1,0:T(8,128)}) %reduce-scatter.2.cloned.1.call-update) | async-done | bytes 565264 | tf_op jit(solution)/shard_map/reduce_scatter | solution.py:277
  152.4 1.1 slice.514
  159.0 1.5 multiply_add_fusion.1
  161.4 15.8 %shard_map.109 = f32[2,128,128]{2,1,0:T(8,128)} custom-call(f32[2,128,128]{2,1,0:T(8,128)} %get-tuple-element.88.d_ref), custom_call_target="tpu_custom_call" | custom-call | flops 50331648 | bytes 262144 | tf_op jit(solution)/shard_map/pallas_call | solution.py:104
  177.7 0.9 pad_maximum_fusion.7
  178.7 1.0 copy.58
  179.7 1.0 copy.67
  180.8 1.0 copy.57
  182.1 1.4 fusion.47
  183.5 2.1 convolution_subtract_fusion
  187.3 15.8 %shard_map.110 = f32[2,128,128]{2,1,0:T(8,128)} custom-call(f32[2,128,128]{2,1,0:T(8,128)} %slice.534.d_ref), custom_call_target="tpu_custom_call" | custom-call | flops 50331648 | bytes 262144 | tf_op jit(solution)/shard_map/pallas_call | solution.py:104
  203.1 1.4 fusion.65
  204.5 1.2 fusion.178
  205.7 1.7 convolution_subtract_fusion.1
  208.8 15.8 %shard_map.111 = f32[2,128,128]{2,1,0:T(8,128)} custom-call(f32[2,128,128]{2,1,0:T(8,128)} %slice.539.d_ref), custom_call_target="tpu_custom_call" | custom-call | flops 50331648 | bytes 262144 | tf_op jit(solution)/shard_map/pallas_call | solution.py:104
  224.6 1.4 fusion.143
  226.0 1.2 fusion.176
  227.3 2.0 convolution_subtract_fusion.2.d_ref
  229.5 15.8 %shard_map.112 = f32[2,128,128]{2,1,0:T(8,128)} custom-call(f32[2,128,128]{2,1,0:T(8,128)} %convolution_subtract_fusion.2.d_ref), custom_call_target="tpu_custom_call" | custom-call | flops 50331648 | bytes 262144 | tf_op jit(solution)/shard_map/pallas_call | solution.py:104
  245.3 1.2 fusion.204
  246.5 1.1 fusion.201
  249.3 21.5 %all_gather.3 = bf16[32,500,16]{1,2,0:T(8,128)(2,1)S(1)} all-gather(bf16[2,500,16]{1,2,0:T(8,128)(2,1)S(1)} %pad_maximum_fusion.9), channel_id=1, replica_groups=mesh['sample'=16,'block'=2] {'sample'}, dimensions={0}, use_global_device_ids=true | all-gather | bytes 544000 | tf_op jit(solution)/shard_map/all_gather | solution.py:307
  273.6 7.0 %all_to_all.18 = bf16[16,4,1024]{2,1,0:T(4,128)(2,1)S(1)} all-to-all(bf16[16,4,1024]{2,1,0:T(4,128)(2,1)S(1)} %pad_maximum_fusion.8), channel_id=1, replica_groups=mesh['sample'=16,'block'=2] {'block'}, dimensions={0} | all-to-all | bytes 262144 | tf_op jit(solution)/shard_map/all_to_all | solution.py:320
  (203 shorter events, 35.2 us)
Async XLA Ops:
  6.5 8.7 %copy-start = (bf16[1024,16]{0,1:T(8,128)(2,1)S(1)}, bf16[1024,16]{0,1:T(8,128)(2,1)}, u32[]{:S(2)}) copy-start(bf16[1024,16]{0,1:T(8,128)(2,1)} %param.21) | copy-start | bytes 98308
  6.5 145.9 %reduce-scatter.2.cloned.1.call-start = ((), (), s32[]{:S(2)}) async-start(), calls=%async_computation.2 | async-start | bytes 9609216 | tf_op jit(solution)/shard_map/reduce_scatter | solution.py:277
  10.0 0.7 copy-start.17
  13.0 2.2 copy-start.10
  13.0 2.3 copy-start.13
  13.0 2.2 copy-start.21
  15.9 6.0 %copy-start.4 = (bf16[1024,512]{0,1:T(8,128)(2,1)S(1)}, bf16[1024,512]{0,1:T(8,128)(2,1)}, u32[]{:S(2)}) copy-start(bf16[1024,512]{0,1:T(8,128)(2,1)} %get-tuple-element.93) | copy-start | bytes 3145732
  21.9 1.4 copy-start.11
  21.9 1.5 copy-start.12
  22.8 2.2 copy-start.3
  25.3 1.4 copy-start.14
  25.3 1.4 copy-start.16
  28.4 0.8 copy-start.23
  34.1 0.7 copy-start.20
  34.1 0.7 copy-start.19
  40.8 0.7 copy-start.22
  40.8 1.3 copy-start.1
  40.8 1.9 copy-start.2
  40.8 4.3 %copy-start.18 = (f32[10]{0:T(128)S(1)}, f32[10]{0:T(128)}, u32[]{:S(2)}) copy-start(f32[10]{0:T(128)} %constant.333) | copy-start | bytes 124
  160.5 16.7 %slice-start = ((f32[1,1104,128]{2,1,0:T(8,128)}), f32[1,64,128]{2,1,0:T(8,128)S(1)}, s32[]{:S(2)}) async-start(f32[1,1104,128]{2,1,0:T(8,128)} %reduce-scatter.2.cloned.1.call-done), calls=%async_computation.3 | async-start | bytes 65536 | tf_op jit(solution)/shard_map/slice | solution.py:281
  177.2 4.6 %copy-start.5 = (f32[2,128,128]{2,1,0:T(8,128)S(1)}, f32[2,128,128]{2,1,0:T(8,128)}, u32[]{:S(2)}) copy-start(f32[2,128,128]{2,1,0:T(8,128)} %shard_map.109) | copy-start | bytes 393220
  181.8 1.7 copy-start.8
  185.6 1.1 copy-start.15
  207.4 0.8 copy-start.9
  207.4 41.0 %copy-start.6 = (f32[2,128,128]{2,1,0:T(8,128)S(1)}, f32[2,128,128]{2,1,0:T(8,128)}, u32[]{:S(2)}) copy-start(f32[2,128,128]{2,1,0:T(8,128)} %shard_map.110) | copy-start | bytes 393220
  224.6 23.3 %copy-start.7 = (f32[2,128,128]{2,1,0:T(8,128)S(1)}, f32[2,128,128]{2,1,0:T(8,128)}, u32[]{:S(2)}) copy-start(f32[2,128,128]{2,1,0:T(8,128)} %shard_map.111) | copy-start | bytes 393220
Sparse Core Ops, SparseCore 0:
  40.9 111.4 reduce-scatter.1
